TPU v7x, 32 devices: a whole 2x2x4 slice. The times are simulated.
32 devices in a mesh: seq: 8 (over y, x, core), head: 4 (over z).
Axes of the slice: x: 2, y: 2, z: 4, core: 2. Of those that a mesh axis runs over, the one named last changes fastest.
Arguments:
- query_rows: bfloat16 [4096, 8192], P(('seq', 'head')), may hold values from -150 to 150
- key_rows: bfloat16 [4096, 1024], P(('seq', 'head')), may hold values from -5 to 5
- value_rows: bfloat16 [4096, 1024], P(('seq', 'head')), may hold values from -6 to 6
- doc_ids: int32 [4096], replicated, may hold values from 0 to 1, never falling along the last dimension, each value on 1 to 3584 neighbouring positions
Outputs:
- attended: bfloat16 [4096, 8192], P(('seq', 'head'))
Inputs may be any that keep to these rules, and one draw needn't show every extreme that they name: `doc_ids`: never falls along the pack; each document has 1 to 3584 tokens.
All inputs are finite; a program needn't handle non-finite values.
Results may differ from a plain program's by a relative error of at most 0.0039.
Values may be sent and summed in bfloat16 or wider, within the bound.
No kernel may reach another device: no remote copies, remote signals or barrier semaphores. Data moves between devices by JAX's collectives and lax.ppermute only.
A program may use at most 128 MiB of HBM per device.

v0:
```python
import functools
import math

import jax
import jax.numpy as jnp
from jax import lax
from jax.experimental import pallas as pl
from jax.experimental.pallas import tpu as pltpu
from jax.sharding import PartitionSpec as P

HEAD_DIM = 128
KEY_ROWS = 512
DOC_MOST = 3584
NEG_START = -1e30


def flash_kernel(meta_ref, doc_ref, q_ref, k_ref, vt_ref, qdoc_ref, kdoc_ref, o_ref, qt_sc, m_sc, l_sc, acc_sc,
                 *, heads_per, groups, q_rows, steps, scale):
    step = pl.program_id(0)
    first_block = meta_ref[0]
    last_block = meta_ref[1]
    q_off = meta_ref[2]
    key_block = jnp.minimum(first_block + step, last_block)
    active = first_block + step <= last_block
    full = (key_block * KEY_ROWS + KEY_ROWS - 1 < q_off) & (
        doc_ref[key_block * KEY_ROWS] == doc_ref[q_off + q_rows - 1]
    )

    @pl.when(step == 0)
    def _():
        m_sc[...] = jnp.full(m_sc.shape, NEG_START, jnp.float32)
        l_sc[...] = jnp.zeros(l_sc.shape, jnp.float32)
        acc_sc[...] = jnp.zeros(acc_sc.shape, jnp.float32)
        for j in range(groups * heads_per):
            cols = slice(j * HEAD_DIM, (j + 1) * HEAD_DIM)
            qt_sc[j] = q_ref[:, cols].astype(jnp.float32).T.astype(jnp.bfloat16)

    def compute(masked):
        if masked:
            key_pos = key_block * KEY_ROWS + lax.broadcasted_iota(jnp.int32, (KEY_ROWS, q_rows), 0)
            query_pos = q_off + lax.broadcasted_iota(jnp.int32, (KEY_ROWS, q_rows), 1)
            visible = (key_pos <= query_pos) & (kdoc_ref[...] == qdoc_ref[0])
        for g in range(groups):
            keys = k_ref[:, g * HEAD_DIM:(g + 1) * HEAD_DIM]
            values_t = vt_ref[g * HEAD_DIM:(g + 1) * HEAD_DIM, :]
            for r in range(heads_per):
                j = g * heads_per + r
                scores = jnp.dot(keys, qt_sc[j], preferred_element_type=jnp.float32)
                if masked:
                    scores = jnp.where(visible, scores, -jnp.inf)
                m_old = m_sc[j]
                m_new = jnp.maximum(m_old, jnp.max(scores, axis=0, keepdims=True))
                weights = jnp.exp2((scores - m_new) * scale)
                factor = jnp.exp2((m_old - m_new) * scale)
                l_sc[j] = l_sc[j] * factor + jnp.sum(weights, axis=0, keepdims=True)
                product = jnp.dot(values_t, weights.astype(jnp.bfloat16), preferred_element_type=jnp.float32)
                acc_sc[j] = acc_sc[j] * factor + product
                m_sc[j] = m_new

    @pl.when(active & full)
    def _():
        compute(False)

    @pl.when(active & jnp.logical_not(full))
    def _():
        compute(True)

    @pl.when(step == steps - 1)
    def _():
        for j in range(groups * heads_per):
            cols = slice(j * HEAD_DIM, (j + 1) * HEAD_DIM)
            o_ref[:, cols] = (acc_sc[j] / l_sc[j]).T.astype(o_ref.dtype)


def attend(q_tile, q_off, keys, values_t, doc_ids, groups, heads_per):
    tokens = doc_ids.shape[0]
    q_rows = q_tile.shape[0]
    blocks = tokens // KEY_ROWS
    steps = min(blocks, -(-DOC_MOST // KEY_ROWS) + 1)
    doc_start = jnp.sum((doc_ids < doc_ids[q_off]).astype(jnp.int32))
    meta = jnp.stack([doc_start // KEY_ROWS, (q_off + q_rows - 1) // KEY_ROWS, q_off]).astype(jnp.int32)
    width = groups * heads_per * HEAD_DIM
    kv_width = groups * HEAD_DIM
    heads = groups * heads_per

    def key_index(j, meta, docs):
        return jnp.minimum(meta[0] + j, meta[1])

    kernel = functools.partial(
        flash_kernel, heads_per=heads_per, groups=groups, q_rows=q_rows, steps=steps,
        scale=math.log2(math.e) / HEAD_DIM**0.5,
    )
    return pl.pallas_call(
        kernel,
        out_shape=jax.ShapeDtypeStruct((q_rows, width), jnp.bfloat16),
        grid_spec=pltpu.PrefetchScalarGridSpec(
            num_scalar_prefetch=2,
            grid=(steps,),
            in_specs=[
                pl.BlockSpec((q_rows, width), lambda j, meta, docs: (0, 0)),
                pl.BlockSpec((KEY_ROWS, kv_width), lambda j, meta, docs: (key_index(j, meta, docs), 0)),
                pl.BlockSpec((kv_width, KEY_ROWS), lambda j, meta, docs: (0, key_index(j, meta, docs))),
                pl.BlockSpec((1, 1, q_rows), lambda j, meta, docs: (meta[2] // q_rows, 0, 0)),
                pl.BlockSpec((KEY_ROWS, 1), lambda j, meta, docs: (key_index(j, meta, docs), 0)),
            ],
            out_specs=pl.BlockSpec((q_rows, width), lambda j, meta, docs: (0, 0)),
            scratch_shapes=[
                pltpu.VMEM((heads, HEAD_DIM, q_rows), jnp.bfloat16),
                pltpu.VMEM((heads, 1, q_rows), jnp.float32),
                pltpu.VMEM((heads, 1, q_rows), jnp.float32),
                pltpu.VMEM((heads, HEAD_DIM, q_rows), jnp.float32),
            ],
        ),
        compiler_params=pltpu.CompilerParams(dimension_semantics=("arbitrary",)),
    )(meta, doc_ids, q_tile, keys, values_t, doc_ids.reshape(tokens // q_rows, 1, q_rows), doc_ids.reshape(tokens, 1))


def gather_kv(key_rows, value_rows):
    stacked = jnp.stack([key_rows, value_rows], axis=1)
    local = lax.all_to_all(stacked, "head", split_axis=2, concat_axis=0, tiled=True)
    whole = lax.all_gather(local, "seq", axis=0, tiled=True)
    return whole[:, 0, :], whole[:, 1, :].T


def body(query_rows, key_rows, value_rows, doc_ids):
    head_count = lax.axis_size("head")
    head = lax.axis_index("head")
    sub = query_rows.shape[0]
    q_width = query_rows.shape[1] // head_count
    groups = key_rows.shape[1] // HEAD_DIM // head_count
    heads_per = query_rows.shape[1] // key_rows.shape[1]
    block_start = lax.axis_index("seq") * sub * head_count
    keys, values_t = gather_kv(key_rows, value_rows)
    result = jnp.zeros_like(query_rows)
    for t in range(head_count):
        piece = lax.dynamic_slice_in_dim(query_rows, ((head + t) % head_count) * q_width, q_width, axis=1)
        if t:
            piece = lax.ppermute(piece, "head", [(i, (i + t) % head_count) for i in range(head_count)])
        q_off = block_start + ((head - t) % head_count) * sub
        out_tile = attend(piece, q_off, keys, values_t, doc_ids, groups, heads_per)
        if t:
            out_tile = lax.ppermute(out_tile, "head", [(i, (i - t) % head_count) for i in range(head_count)])
        result = lax.dynamic_update_slice_in_dim(result, out_tile, ((head + t) % head_count) * q_width, axis=1)
    return result


def solution(mesh):
    placed = (P(("seq", "head"), None), P(("seq", "head"), None), P(("seq", "head"), None), P())
    return jax.shard_map(
        body, mesh=mesh, in_specs=placed, out_specs=P(("seq", "head"), None), check_vma=False
    )
```

profile of v0, /device:TPU:7, one launch (start us, length us, event | category | flops | bytes accessed | tf_op | source)
XLA Modules:
  0.0 144.0 jit_solution(7343030606362534445)
XLA Ops:
  6.5 0.0 all-gather.2.cloned.1.call-start
  6.5 1.1 pad_maximum_fusion
  7.6 0.4 copy.30
  8.0 0.0 copy-start.1
  8.1 18.2 %all_to_all.18 = bf16[128,2,1024]{0,1,2:T(2,128)(2,1)S(1)} all-to-all(bf16[128,2,1024]{0,1,2:T(2,128)(2,1)S(1)} %copy.30), channel_id=1, replica_groups=mesh['seq'=8,'head'=4] {'head'}, dimensions={2} | all-to-all | bytes 1048576 | tf_op jit(solution)/shard_map/all_to_all | solution.py:120
  26.2 0.4 copy.41
  26.6 1.0 all_to_all.16
  27.6 0.0 all-gather.2.cloned.1.call-update
  27.7 0.0 copy-done.1
  27.7 0.0 copy-start.3
  27.7 1.3 constant_dynamic-slice_fusion
  29.0 1.8 %collective-permute-start.4 = (bf16[128,2048]{1,0:T(8,128)(2,1)S(1)}, bf16[128,2048]{1,0:T(8,128)(2,1)S(1)}, u32[]{:S(2)}, u32[]{:S(2)}) collective-permute-start(bf16[128,2048]{1,0:T(8,128)(2,1)S(1)} %get-tuple-element.11), channel_id=1, source_target_pairs={{0,3},{1,0},{2,1},{3,2},{4,7},{5,4},{6,5},{7,6},{8,11},{9,8},{10,9... | collective-permute-start | bytes 1572872 | tf_op jit(solution)/shard_map/ppermute | solution.py:138
  30.8 0.0 collective-permute-start.2
  30.8 0.3 collective-permute-start
  31.1 0.0 copy-done.3
  31.1 0.6 fusion
  31.7 3.1 %convert_reduce_fusion = (s32[]{:T(128)}, s32[]{:T(128)}, s32[]{:T(128)}, s32[]{:T(128)}) fusion(s32[4096]{0:T(1024)S(1)} %copy-done.3, s32[]{:T(128)} %bitcast.22, s32[]{:T(128)} %bitcast.18, s32[]{:T(128)} %bitcast.13, s32[]{:T(128)} %bitcast), kind=kLoop, calls=%fused_computation.4 | loop fusion | flops 49148 | bytes 16416 | tf_op jit(solution)/shard_map/reduce_sum | solution.py:80
  45.4 2.0 %copy.33.kdoc_ref = s32[4096,1]{1,0:T(8,128)} copy(s32[4096,1]{0,1:T(1,128)S(1)} %bitcast.38) | data formatting | bytes 32768 | tf_op jit(solution)/shard_map/reshape | solution.py:115
  47.4 0.6 pad_add_fusion.1.meta_ref
  48.0 17.0 %all-gather.2.cloned.1.call-done = bf16[4096,2,256]{0,2,1:T(8,128)(2,1)} async-done(((bf16[512,2,256]{0,2,1:T(8,128)(2,1)}), bf16[4096,2,256]{0,2,1:T(8,128)(2,1)}) %all-gather.2.cloned.1.call-update) | async-done | bytes 4194320 | tf_op jit(solution)/shard_map/all_gather | solution.py:121
  65.1 3.9 %slice_bitcast_fusion = (bf16[256,4096]{1,0:T(8,128)(2,1)}, bf16[4096,256]{0,1:T(8,128)(2,1)S(1)}) fusion(bf16[4096,2,256]{0,2,1:T(8,128)(2,1)} %all-gather.2.cloned.1.call-done), kind=kLoop, calls=%fused_computation | loop fusion | bytes 8388608 | tf_op jit(solution)/shard_map/transpose | solution.py:122
  69.0 2.5 %copy.32.k_ref = bf16[4096,256]{1,0:T(8,128)(2,1)} copy(bf16[4096,256]{0,1:T(8,128)(2,1)S(1)} %get-tuple-element.10) | data formatting | bytes 4194304 | tf_op jit(solution)/shard_map/squeeze | solution.py:122
  71.5 0.0 collective-permute-done.q_ref
  71.5 11.1 %shard_map.47 = bf16[128,2048]{1,0:T(8,128)(2,1)} custom-call(s32[3]{0:T(128)} %pad_add_fusion.1.meta_ref, s32[4096]{0:T(1024)} %doc_ref.7, bf16[128,2048]{1,0:T(8,128)(2,1)} %collective-permute-done.q_ref, bf16[4096,256]{1,0:T(8,128)(2,1)} %copy.32.k_ref, bf16[256,4096]{1,0:T(8,128)(2,1)} %get-tuple-element.9.vt_ref, s32[32,1,128]{2,1,0:T(1,128)} %bitcast.34, ...), custom_call_target="tpu_custom_call" | custom-call | tf_op jit(solution)/shard_map/pallas_call | solution.py:93
  82.6 3.0 %collective-permute-start.1 = (bf16[128,2048]{1,0:T(8,128)(2,1)}, bf16[128,2048]{1,0:T(8,128)(2,1)S(1)}, u32[]{:S(2)}, u32[]{:S(2)}) collective-permute-start(bf16[128,2048]{1,0:T(8,128)(2,1)} %shard_map.47), channel_id=1, source_target_pairs={{0,3},{1,0},{2,1},{3,2},{4,7},{5,4},{6,5},{7,6},{8,11},{9,8},{10,9... | collective-permute-start | bytes 1572872 | tf_op jit(solution)/shard_map/ppermute | solution.py:142
  85.6 0.6 pad_add_fusion.3.meta_ref
  86.2 0.6 pad_add_fusion.2.meta_ref
  86.7 0.0 collective-permute-done.2.q_ref
  86.7 11.1 %shard_map.48 = bf16[128,2048]{1,0:T(8,128)(2,1)} custom-call(s32[3]{0:T(128)} %pad_add_fusion.2.meta_ref, s32[4096]{0:T(1024)} %doc_ref.7, bf16[128,2048]{1,0:T(8,128)(2,1)} %collective-permute-done.2.q_ref, bf16[4096,256]{1,0:T(8,128)(2,1)} %copy.32.k_ref, bf16[256,4096]{1,0:T(8,128)(2,1)} %get-tuple-element.9.vt_ref, s32[32,1,128]{2,1,0:T(1,128)} %bitcast.35, ...), custom_call_target="tpu_custom_call" | custom-call | tf_op jit(solution)/shard_map/pallas_call | solution.py:93
  97.8 3.5 %collective-permute-start.3 = (bf16[128,2048]{1,0:T(8,128)(2,1)}, bf16[128,2048]{1,0:T(8,128)(2,1)S(1)}, u32[]{:S(2)}, u32[]{:S(2)}) collective-permute-start(bf16[128,2048]{1,0:T(8,128)(2,1)} %shard_map.48), channel_id=1, source_target_pairs={{0,2},{1,3},{2,0},{3,1},{4,6},{5,7},{6,4},{7,5},{8,10},{9,11},{10,... | collective-permute-start | bytes 1572872 | tf_op jit(solution)/shard_map/ppermute | solution.py:142
  101.3 0.7 pad_add_fusion.meta_ref
  102.0 0.0 collective-permute-done.4.q_ref
  102.0 0.0 copy-start.4
  102.0 0.8 copy-done.4
  102.8 11.0 %shard_map.49 = bf16[128,2048]{1,0:T(8,128)(2,1)} custom-call(s32[3]{0:T(128)} %pad_add_fusion.3.meta_ref, s32[4096]{0:T(1024)} %doc_ref.7, bf16[128,2048]{1,0:T(8,128)(2,1)} %copy-done.4, bf16[4096,256]{1,0:T(8,128)(2,1)} %copy.32.k_ref, bf16[256,4096]{1,0:T(8,128)(2,1)} %get-tuple-element.9.vt_ref, s32[32,1,128]{2,1,0:T(1,128)} %bitcast.36, ...), custom_call_target="tpu_custom_call" | custom-call | tf_op jit(solution)/shard_map/pallas_call | solution.py:93
  113.9 1.5 %collective-permute-start.5 = (bf16[128,2048]{1,0:T(8,128)(2,1)}, bf16[128,2048]{1,0:T(8,128)(2,1)S(1)}, u32[]{:S(2)}, u32[]{:S(2)}) collective-permute-start(bf16[128,2048]{1,0:T(8,128)(2,1)} %shard_map.49), channel_id=1, source_target_pairs={{0,1},{1,2},{2,3},{3,0},{4,5},{5,6},{6,7},{7,4},{8,9},{9,10},{10,1... | collective-permute-start | bytes 1572872 | tf_op jit(solution)/shard_map/ppermute | solution.py:142
  115.3 11.1 %shard_map.46 = bf16[128,2048]{1,0:T(8,128)(2,1)} custom-call(s32[3]{0:T(128)} %pad_add_fusion.meta_ref, s32[4096]{0:T(1024)} %doc_ref.7, bf16[128,2048]{1,0:T(8,128)(2,1)} %get-tuple-element.13.q_ref, bf16[4096,256]{1,0:T(8,128)(2,1)} %copy.32.k_ref, bf16[256,4096]{1,0:T(8,128)(2,1)} %get-tuple-element.9.vt_ref, s32[32,1,128]{2,1,0:T(1,128)} %bitcast.37, ...), custom_call_target="tpu_custom_call" | custom-call | tf_op jit(solution)/shard_map/pallas_call | solution.py:93
  126.4 0.0 copy-start.2
  126.4 0.2 broadcast_in_dim.3
  126.6 0.8 copy-done.2
  127.5 0.0 collective-permute-done.1
  127.6 7.4 %collective-permute-done.3 = bf16[128,2048]{1,0:T(8,128)(2,1)S(1)} collective-permute-done((bf16[128,2048]{1,0:T(8,128)(2,1)}, bf16[128,2048]{1,0:T(8,128)(2,1)S(1)}, u32[]{:S(2)}, u32[]{:S(2)}) %collective-permute-start.3) | collective-permute-done | bytes 524320 | tf_op jit(solution)/shard_map/ppermute | solution.py:142
  135.0 0.0 copy-start
  135.1 0.0 collective-permute-done.5
  135.1 1.3 copy-done
  136.4 0.8 constant_dynamic-update-slice_fusion
  (3 shorter events, 0.1 us)
Async XLA Ops:
  6.5 58.5 %all-gather.2.cloned.1.call-start = ((), (), s32[]{:S(2)}) async-start(), calls=%async_computation.1 | async-start | bytes 4718592 | tf_op jit(solution)/shard_map/all_gather | solution.py:121
  8.0 19.7 %copy-start.1 = (bf16[128,8192]{1,0:T(8,128)(2,1)S(1)}, bf16[128,8192]{1,0:T(8,128)(2,1)}, u32[]{:S(2)}) copy-start(bf16[128,8192]{1,0:T(8,128)(2,1)} %param.4) | copy-start | bytes 6291460
  27.7 3.4 %copy-start.3 = (s32[4096]{0:T(1024)S(1)}, s32[4096]{0:T(1024)}, u32[]{:S(2)}) copy-start(s32[4096]{0:T(1024)} %doc_ref.7) | copy-start | bytes 49156
  29.0 73.0 %collective-permute-start.4 = (bf16[128,2048]{1,0:T(8,128)(2,1)S(1)}, bf16[128,2048]{1,0:T(8,128)(2,1)S(1)}, u32[]{:S(2)}, u32[]{:S(2)}) collective-permute-start(bf16[128,2048]{1,0:T(8,128)(2,1)S(1)} %get-tuple-element.11), channel_id=1, source_target_pairs={{0,3},{1,0},{2,1},{3,2},{4,7},{5,4},{6,5},{7,6},{8,11},{9,8},{10,9... | collective-permute-start | bytes 1572872 | tf_op jit(solution)/shard_map/ppermute | solution.py:138
  30.8 55.9 %collective-permute-start.2 = (bf16[128,2048]{1,0:T(8,128)(2,1)}, bf16[128,2048]{1,0:T(8,128)(2,1)}, u32[]{:S(2)}, u32[]{:S(2)}) collective-permute-start(bf16[128,2048]{1,0:T(8,128)(2,1)} %get-tuple-element.14), channel_id=1, source_target_pairs={{0,2},{1,3},{2,0},{3,1},{4,6},{5,7},{6,4},{7,5},{8,10},{9,11},{10,... | collective-permute-start | bytes 1572872 | tf_op jit(solution)/shard_map/ppermute | solution.py:138
  30.8 40.6 %collective-permute-start = (bf16[128,2048]{1,0:T(8,128)(2,1)}, bf16[128,2048]{1,0:T(8,128)(2,1)}, u32[]{:S(2)}, u32[]{:S(2)}) collective-permute-start(bf16[128,2048]{1,0:T(8,128)(2,1)} %get-tuple-element.12), channel_id=1, source_target_pairs={{0,1},{1,2},{2,3},{3,0},{4,5},{5,6},{6,7},{7,4},{8,9},{9,10},{10,1... | collective-permute-start | bytes 1572872 | tf_op jit(solution)/shard_map/ppermute | solution.py:138
  82.6 44.9 %collective-permute-start.1 = (bf16[128,2048]{1,0:T(8,128)(2,1)}, bf16[128,2048]{1,0:T(8,128)(2,1)S(1)}, u32[]{:S(2)}, u32[]{:S(2)}) collective-permute-start(bf16[128,2048]{1,0:T(8,128)(2,1)} %shard_map.47), channel_id=1, source_target_pairs={{0,3},{1,0},{2,1},{3,2},{4,7},{5,4},{6,5},{7,6},{8,11},{9,8},{10,9... | collective-permute-start | bytes 1572872 | tf_op jit(solution)/shard_map/ppermute | solution.py:142
  97.8 37.2 %collective-permute-start.3 = (bf16[128,2048]{1,0:T(8,128)(2,1)}, bf16[128,2048]{1,0:T(8,128)(2,1)S(1)}, u32[]{:S(2)}, u32[]{:S(2)}) collective-permute-start(bf16[128,2048]{1,0:T(8,128)(2,1)} %shard_map.48), channel_id=1, source_target_pairs={{0,2},{1,3},{2,0},{3,1},{4,6},{5,7},{6,4},{7,5},{8,10},{9,11},{10,... | collective-permute-start | bytes 1572872 | tf_op jit(solution)/shard_map/ppermute | solution.py:142
  102.0 0.8 copy-start.4
  113.9 21.2 %collective-permute-start.5 = (bf16[128,2048]{1,0:T(8,128)(2,1)}, bf16[128,2048]{1,0:T(8,128)(2,1)S(1)}, u32[]{:S(2)}, u32[]{:S(2)}) collective-permute-start(bf16[128,2048]{1,0:T(8,128)(2,1)} %shard_map.49), channel_id=1, source_target_pairs={{0,1},{1,2},{2,3},{3,0},{4,5},{5,6},{6,7},{7,4},{8,9},{9,10},{10,1... | collective-permute-start | bytes 1572872 | tf_op jit(solution)/shard_map/ppermute | solution.py:142
  126.4 1.0 copy-start.2
  135.0 1.3 copy-start
Sparse Core Ops, SparseCore 0:
  27.8 37.2 all-gather.1
where the time goes:
time: 146 us; the launch traced here: 144 us
  Pallas kernels  44.3 us (30%)
  waiting for transfers between devices  24.5 us (17%)
  between operations  24.1 us (17%)
  blocking collectives  18.2 us (12%)
  local copies, waits for them, and re-layouts  16.2 us (11%)
  starting transfers between devices  10.1 us (7%)
  other arithmetic  6.64 us (5%)
    pallas_call x4, Pallas kernels, attend(): pl.pallas_call(kernel, out_shape=jax.ShapeDtypeStruct((q_rows, width), jn...  44.3 us
    all_to_all x1, blocking collectives, gather_kv(): lax.all_to_all(stacked, 'head', split_axis=2, concat_axis=0, tiled=True)  18.2 us
    all_gather x1, waiting for transfers between devices, gather_kv(): whole = lax.all_gather(local, 'seq', axis=0, tiled=True)  17 us
    ppermute x3, starting transfers between devices, body(): lax.ppermute(out_tile, 'head', [(i, (i - t) % head_count) for i in range(...  8 us
    ppermute x3, waiting for transfers between devices, body(): lax.ppermute(out_tile, 'head', [(i, (i - t) % head_count) for i in range(...  7.44 us
    transpose x1, local copies, waits for them, and re-layouts, gather_kv(): return (whole[:, 0, :], whole[:, 1, :].T)  3.92 us
    reduce_sum x1, other arithmetic, attend(): doc_start = jnp.sum((doc_ids < doc_ids[q_off]).astype(jnp.int32))  3.15 us
    unnamed x10, local copies, waits for them, and re-layouts  2.96 us
  transfers between devices with their start and end apart: 7, of which 2 were waited for; matrix products, arithmetic and copies ran while one was open for 11% of the time, Pallas kernels for 31%

commit v1 on v0

--- a/solution.py
+++ b/solution.py
@@ -14,7 +14,7 @@
 NEG_START = -1e30
 
 
-def flash_kernel(meta_ref, doc_ref, q_ref, k_ref, vt_ref, qdoc_ref, kdoc_ref, o_ref, qt_sc, m_sc, l_sc, acc_sc,
+def flash_kernel(meta_ref, doc_ref, q_ref, k_ref, vt_ref, qstart_ref, o_ref, qt_sc, m_sc, l_sc, acc_sc,
                  *, heads_per, groups, q_rows, steps, scale):
     step = pl.program_id(0)
     first_block = meta_ref[0]
@@ -39,7 +39,7 @@
         if masked:
             key_pos = key_block * KEY_ROWS + lax.broadcasted_iota(jnp.int32, (KEY_ROWS, q_rows), 0)
             query_pos = q_off + lax.broadcasted_iota(jnp.int32, (KEY_ROWS, q_rows), 1)
-            visible = (key_pos <= query_pos) & (kdoc_ref[...] == qdoc_ref[0])
+            visible = (key_pos <= query_pos) & (key_pos >= qstart_ref[...])
         for g in range(groups):
             keys = k_ref[:, g * HEAD_DIM:(g + 1) * HEAD_DIM]
             values_t = vt_ref[g * HEAD_DIM:(g + 1) * HEAD_DIM, :]
@@ -77,8 +77,9 @@
     q_rows = q_tile.shape[0]
     blocks = tokens // KEY_ROWS
     steps = min(blocks, -(-DOC_MOST // KEY_ROWS) + 1)
-    doc_start = jnp.sum((doc_ids < doc_ids[q_off]).astype(jnp.int32))
-    meta = jnp.stack([doc_start // KEY_ROWS, (q_off + q_rows - 1) // KEY_ROWS, q_off]).astype(jnp.int32)
+    query_doc = lax.dynamic_slice_in_dim(doc_ids, q_off, q_rows)
+    query_start = jnp.sum((doc_ids[None, :] < query_doc[:, None]).astype(jnp.int32), axis=1).reshape(1, q_rows)
+    meta = jnp.stack([query_start[0, 0] // KEY_ROWS, (q_off + q_rows - 1) // KEY_ROWS, q_off]).astype(jnp.int32)
     width = groups * heads_per * HEAD_DIM
     kv_width = groups * HEAD_DIM
     heads = groups * heads_per
@@ -100,8 +101,7 @@
                 pl.BlockSpec((q_rows, width), lambda j, meta, docs: (0, 0)),
                 pl.BlockSpec((KEY_ROWS, kv_width), lambda j, meta, docs: (key_index(j, meta, docs), 0)),
                 pl.BlockSpec((kv_width, KEY_ROWS), lambda j, meta, docs: (0, key_index(j, meta, docs))),
-                pl.BlockSpec((1, 1, q_rows), lambda j, meta, docs: (meta[2] // q_rows, 0, 0)),
-                pl.BlockSpec((KEY_ROWS, 1), lambda j, meta, docs: (key_index(j, meta, docs), 0)),
+                pl.BlockSpec((1, q_rows), lambda j, meta, docs: (0, 0)),
             ],
             out_specs=pl.BlockSpec((q_rows, width), lambda j, meta, docs: (0, 0)),
             scratch_shapes=[
@@ -112,12 +112,21 @@
             ],
         ),
         compiler_params=pltpu.CompilerParams(dimension_semantics=("arbitrary",)),
-    )(meta, doc_ids, q_tile, keys, values_t, doc_ids.reshape(tokens // q_rows, 1, q_rows), doc_ids.reshape(tokens, 1))
+    )(meta, doc_ids, q_tile, keys, values_t, query_start)
 
 
 def gather_kv(key_rows, value_rows):
+    head_count = lax.axis_size("head")
+    head = lax.axis_index("head")
+    sub = key_rows.shape[0]
+    width = key_rows.shape[1] // head_count
     stacked = jnp.stack([key_rows, value_rows], axis=1)
-    local = lax.all_to_all(stacked, "head", split_axis=2, concat_axis=0, tiled=True)
+    local = jnp.zeros((head_count * sub, 2, width), stacked.dtype)
+    for t in range(head_count):
+        piece = lax.dynamic_slice_in_dim(stacked, ((head + t) % head_count) * width, width, axis=2)
+        if t:
+            piece = lax.ppermute(piece, "head", [(i, (i + t) % head_count) for i in range(head_count)])
+        local = lax.dynamic_update_slice_in_dim(local, piece, ((head - t) % head_count) * sub, axis=0)
     whole = lax.all_gather(local, "seq", axis=0, tiled=True)
     return whole[:, 0, :], whole[:, 1, :].T
 

time: 146 us -> 147 us (level)
  the two profiles are of different devices: /device:TPU:7 before, /device:TPU:5 now
where the time goes in v1:
time: 147 us
  Pallas kernels  55.6 us (38%)
  waiting for transfers between devices  40.6 us (28%)
  starting transfers between devices  16.4 us (11%)
  local copies, waits for them, and re-layouts  16.1 us (11%)
  between operations  14.4 us (10%)
  other arithmetic  3.46 us (2%)
    pallas_call x4, Pallas kernels, attend(): pl.pallas_call(kernel, out_shape=jax.ShapeDtypeStruct((q_rows, width), jn...  55.6 us
    all_gather x1, waiting for transfers between devices, gather_kv(): whole = lax.all_gather(local, 'seq', axis=0, tiled=True)  31.2 us
    ppermute x3, waiting for transfers between devices, gather_kv(): lax.ppermute(piece, 'head', [(i, (i + t) % head_count) for i in range(hea...  8.19 us
    ppermute x3, starting transfers between devices, body(): lax.ppermute(out_tile, 'head', [(i, (i - t) % head_count) for i in range(...  7.47 us
    unnamed x24, local copies, waits for them, and re-layouts  6.95 us
    ppermute x3, starting transfers between devices, gather_kv(): lax.ppermute(piece, 'head', [(i, (i + t) % head_count) for i in range(hea...  4.73 us
    ppermute x3, starting transfers between devices, body(): lax.ppermute(piece, 'head', [(i, (i + t) % head_count) for i in range(hea...  4.22 us
    transpose x1, local copies, waits for them, and re-layouts, gather_kv(): return (whole[:, 0, :], whole[:, 1, :].T)  3.92 us
  transfers between devices with their start and end apart: 10, of which 4 were waited for; matrix products, arithmetic and copies ran while one was open for 8% of the time, Pallas kernels for 38%

profile of v1, /device:TPU:5, one launch (start us, length us, event | category | flops | bytes accessed | tf_op | source)
XLA Modules:
  0.0 146.6 jit_solution(12490470398805138385)
XLA Ops:
  6.5 1.3 copy.11
  7.8 1.1 copy.12
  9.0 0.1 fusion
  9.1 1.3 collective-permute-start
  10.4 2.3 %collective-permute-start.1 = (bf16[128,2,256]{0,2,1:T(8,128)(2,1)S(1)}, bf16[128,2,256]{0,2,1:T(8,128)(2,1)S(1)}, u32[]{:S(2)}, u32[]{:S(2)}) collective-permute-start(bf16[128,2,256]{0,2,1:T(8,128)(2,1)S(1)} %get-tuple-element.18), channel_id=1, source_target_pairs={{0,2},{1,3},{2,0},{3,1},{4,6},{5,7},{6,4},{7,5},{8,10},{9,11},{10,... | collective-permute-start | bytes 393224 | tf_op jit(solution)/shard_map/ppermute | solution.py:128
  12.8 1.1 collective-permute-start.2
  13.8 1.6 %collective-permute-done = bf16[128,2,256]{0,2,1:T(8,128)(2,1)S(1)} collective-permute-done((bf16[128,2,256]{0,2,1:T(8,128)(2,1)S(1)}, bf16[128,2,256]{0,2,1:T(8,128)(2,1)S(1)}, u32[]{:S(2)}, u32[]{:S(2)}) %collective-permute-start) | collective-permute-done | bytes 131104 | tf_op jit(solution)/shard_map/ppermute | solution.py:128
  15.5 6.6 %collective-permute-done.1 = bf16[128,2,256]{0,2,1:T(8,128)(2,1)S(1)} collective-permute-done((bf16[128,2,256]{0,2,1:T(8,128)(2,1)S(1)}, bf16[128,2,256]{0,2,1:T(8,128)(2,1)S(1)}, u32[]{:S(2)}, u32[]{:S(2)}) %collective-permute-start.1) | collective-permute-done | bytes 131104 | tf_op jit(solution)/shard_map/ppermute | solution.py:128
  22.1 0.0 collective-permute-done.2
  22.1 0.0 copy-start.2
  22.1 0.8 copy-done.2
  22.9 0.0 all-gather.2.cloned.1.call-update
  23.0 0.0 copy-start.6
  23.0 1.4 constant_dynamic-slice_fusion
  24.4 3.1 %collective-permute-start.7 = (bf16[128,2048]{1,0:T(8,128)(2,1)}, bf16[128,2048]{1,0:T(8,128)(2,1)S(1)}, u32[]{:S(2)}, u32[]{:S(2)}) collective-permute-start(bf16[128,2048]{1,0:T(8,128)(2,1)} %get-tuple-element.11), channel_id=1, source_target_pairs={{0,3},{1,0},{2,1},{3,2},{4,7},{5,4},{6,5},{7,6},{8,11},{9,8},{10,9... | collective-permute-start | bytes 1572872 | tf_op jit(solution)/shard_map/ppermute | solution.py:147
  27.5 1.1 collective-permute-start.5
  28.6 0.0 collective-permute-start.3
  28.6 0.0 copy-done.6
  28.6 0.1 fusion.5
  28.7 1.0 convert_reduce_fusion
  29.7 0.0 copy-start.8
  30.4 0.6 pad_add_fusion.1.meta_ref
  31.0 31.2 %all-gather.2.cloned.1.call-done = bf16[4096,2,256]{0,2,1:T(8,128)(2,1)} async-done(((bf16[512,2,256]{0,2,1:T(8,128)(2,1)}), bf16[4096,2,256]{0,2,1:T(8,128)(2,1)}) %all-gather.2.cloned.1.call-update) | async-done | bytes 4194320 | tf_op jit(solution)/shard_map/all_gather | solution.py:130
  62.2 3.9 %slice_bitcast_fusion = (bf16[256,4096]{1,0:T(8,128)(2,1)}, bf16[4096,256]{0,1:T(8,128)(2,1)S(1)}) fusion(bf16[4096,2,256]{0,2,1:T(8,128)(2,1)} %all-gather.2.cloned.1.call-done), kind=kLoop, calls=%fused_computation | loop fusion | bytes 8388608 | tf_op jit(solution)/shard_map/transpose | solution.py:131
  66.1 2.5 %copy.13.k_ref = bf16[4096,256]{1,0:T(8,128)(2,1)} copy(bf16[4096,256]{0,1:T(8,128)(2,1)S(1)} %get-tuple-element.10) | data formatting | bytes 4194304 | tf_op jit(solution)/shard_map/squeeze | solution.py:131
  68.6 0.0 collective-permute-done.3.q_ref
  68.6 13.9 %shard_map.47 = bf16[128,2048]{1,0:T(8,128)(2,1)} custom-call(s32[3]{0:T(128)} %pad_add_fusion.1.meta_ref, s32[4096]{0:T(1024)} %doc_ref.7, bf16[128,2048]{1,0:T(8,128)(2,1)} %collective-permute-done.3.q_ref, bf16[4096,256]{1,0:T(8,128)(2,1)} %copy.13.k_ref, bf16[256,4096]{1,0:T(8,128)(2,1)} %get-tuple-element.9.vt_ref, s32[1,128]{1,0:T(1,128)} %bitcast.53), custom_call_target="tpu_custom_call" | custom-call | tf_op jit(solution)/shard_map/pallas_call | solution.py:94
  82.5 3.1 %collective-permute-start.4 = (bf16[128,2048]{1,0:T(8,128)(2,1)}, bf16[128,2048]{1,0:T(8,128)(2,1)S(1)}, u32[]{:S(2)}, u32[]{:S(2)}) collective-permute-start(bf16[128,2048]{1,0:T(8,128)(2,1)} %shard_map.47), channel_id=1, source_target_pairs={{0,3},{1,0},{2,1},{3,2},{4,7},{5,4},{6,5},{7,6},{8,11},{9,8},{10,9... | collective-permute-start | bytes 1572872 | tf_op jit(solution)/shard_map/ppermute | solution.py:151
  85.6 0.6 pad_add_fusion.3.meta_ref
  86.2 0.6 pad_add_fusion.2.meta_ref
  86.7 0.0 collective-permute-done.5.q_ref
  86.7 0.8 copy-done.5
  87.5 13.9 %shard_map.48 = bf16[128,2048]{1,0:T(8,128)(2,1)} custom-call(s32[3]{0:T(128)} %pad_add_fusion.2.meta_ref, s32[4096]{0:T(1024)} %doc_ref.7, bf16[128,2048]{1,0:T(8,128)(2,1)} %copy-done.5, bf16[4096,256]{1,0:T(8,128)(2,1)} %copy.13.k_ref, bf16[256,4096]{1,0:T(8,128)(2,1)} %get-tuple-element.9.vt_ref, s32[1,128]{1,0:T(1,128)} %bitcast.48), custom_call_target="tpu_custom_call" | custom-call | tf_op jit(solution)/shard_map/pallas_call | solution.py:94
  101.4 3.0 %collective-permute-start.6 = (bf16[128,2048]{1,0:T(8,128)(2,1)}, bf16[128,2048]{1,0:T(8,128)(2,1)S(1)}, u32[]{:S(2)}, u32[]{:S(2)}) collective-permute-start(bf16[128,2048]{1,0:T(8,128)(2,1)} %shard_map.48), channel_id=1, source_target_pairs={{0,2},{1,3},{2,0},{3,1},{4,6},{5,7},{6,4},{7,5},{8,10},{9,11},{10,... | collective-permute-start | bytes 1572872 | tf_op jit(solution)/shard_map/ppermute | solution.py:151
  104.4 0.7 pad_add_fusion.meta_ref
  105.1 0.0 collective-permute-done.7.q_ref
  105.1 0.8 copy-done.4
  105.9 13.9 %shard_map.49 = bf16[128,2048]{1,0:T(8,128)(2,1)} custom-call(s32[3]{0:T(128)} %pad_add_fusion.3.meta_ref, s32[4096]{0:T(1024)} %doc_ref.7, bf16[128,2048]{1,0:T(8,128)(2,1)} %copy-done.4, bf16[4096,256]{1,0:T(8,128)(2,1)} %copy.13.k_ref, bf16[256,4096]{1,0:T(8,128)(2,1)} %get-tuple-element.9.vt_ref, s32[1,128]{1,0:T(1,128)} %bitcast.43), custom_call_target="tpu_custom_call" | custom-call | tf_op jit(solution)/shard_map/pallas_call | solution.py:94
  119.7 1.5 %collective-permute-start.8 = (bf16[128,2048]{1,0:T(8,128)(2,1)}, bf16[128,2048]{1,0:T(8,128)(2,1)S(1)}, u32[]{:S(2)}, u32[]{:S(2)}) collective-permute-start(bf16[128,2048]{1,0:T(8,128)(2,1)} %shard_map.49), channel_id=1, source_target_pairs={{0,1},{1,2},{2,3},{3,0},{4,5},{5,6},{6,7},{7,4},{8,9},{9,10},{10,1... | collective-permute-start | bytes 1572872 | tf_op jit(solution)/shard_map/ppermute | solution.py:151
  121.2 13.9 %shard_map.46 = bf16[128,2048]{1,0:T(8,128)(2,1)} custom-call(s32[3]{0:T(128)} %pad_add_fusion.meta_ref, s32[4096]{0:T(1024)} %doc_ref.7, bf16[128,2048]{1,0:T(8,128)(2,1)} %get-tuple-element.13.q_ref, bf16[4096,256]{1,0:T(8,128)(2,1)} %copy.13.k_ref, bf16[256,4096]{1,0:T(8,128)(2,1)} %get-tuple-element.9.vt_ref, s32[1,128]{1,0:T(1,128)} %bitcast.38), custom_call_target="tpu_custom_call" | custom-call | tf_op jit(solution)/shard_map/pallas_call | solution.py:94
  135.1 0.2 broadcast_in_dim.4
  135.3 0.8 copy-done.1
  136.2 0.0 collective-permute-done.4
  136.3 1.2 collective-permute-done.6
  137.6 0.0 copy-start
  137.6 0.0 collective-permute-done.8
  137.6 1.3 copy-done
  138.9 0.8 constant_dynamic-update-slice_fusion
  (20 shorter events, 0.3 us)
Async XLA Ops:
  6.5 55.6 %all-gather.2.cloned.1.call-start = ((), (), s32[]{:S(2)}) async-start(), calls=%async_computation | async-start | bytes 4718592 | tf_op jit(solution)/shard_map/all_gather | solution.py:130
  6.5 16.5 %copy-start.3 = (bf16[128,8192]{1,0:T(8,128)(2,1)S(1)}, bf16[128,8192]{1,0:T(8,128)(2,1)}, u32[]{:S(2)}) copy-start(bf16[128,8192]{1,0:T(8,128)(2,1)} %param.4) | copy-start | bytes 6291460
  9.1 6.4 %collective-permute-start = (bf16[128,2,256]{0,2,1:T(8,128)(2,1)S(1)}, bf16[128,2,256]{0,2,1:T(8,128)(2,1)S(1)}, u32[]{:S(2)}, u32[]{:S(2)}) collective-permute-start(bf16[128,2,256]{0,2,1:T(8,128)(2,1)S(1)} %get-tuple-element.17), channel_id=1, source_target_pairs={{0,1},{1,2},{2,3},{3,0},{4,5},{5,6},{6,7},{7,4},{8,9},{9,10},{10,1... | collective-permute-start | bytes 393224 | tf_op jit(solution)/shard_map/ppermute | solution.py:128
  10.4 11.6 %collective-permute-start.1 = (bf16[128,2,256]{0,2,1:T(8,128)(2,1)S(1)}, bf16[128,2,256]{0,2,1:T(8,128)(2,1)S(1)}, u32[]{:S(2)}, u32[]{:S(2)}) collective-permute-start(bf16[128,2,256]{0,2,1:T(8,128)(2,1)S(1)} %get-tuple-element.18), channel_id=1, source_target_pairs={{0,2},{1,3},{2,0},{3,1},{4,6},{5,7},{6,4},{7,5},{8,10},{9,11},{10,... | collective-permute-start | bytes 393224 | tf_op jit(solution)/shard_map/ppermute | solution.py:128
  12.8 9.3 %collective-permute-start.2 = (bf16[128,2,256]{0,2,1:T(8,128)(2,1)S(1)}, bf16[128,2,256]{0,2,1:T(8,128)(2,1)S(1)}, u32[]{:S(2)}, u32[]{:S(2)}) collective-permute-start(bf16[128,2,256]{0,2,1:T(8,128)(2,1)S(1)} %get-tuple-element.15), channel_id=1, source_target_pairs={{0,3},{1,0},{2,1},{3,2},{4,7},{5,4},{6,5},{7,6},{8,11},{9,8},{10,9... | collective-permute-start | bytes 393224 | tf_op jit(solution)/shard_map/ppermute | solution.py:128
  22.1 0.8 copy-start.2
  23.0 5.6 %copy-start.6 = (s32[4096]{0:T(1024)S(1)}, s32[4096]{0:T(1024)}, u32[]{:S(2)}) copy-start(s32[4096]{0:T(1024)} %doc_ref.7) | copy-start | bytes 49156
  24.4 80.7 %collective-permute-start.7 = (bf16[128,2048]{1,0:T(8,128)(2,1)}, bf16[128,2048]{1,0:T(8,128)(2,1)S(1)}, u32[]{:S(2)}, u32[]{:S(2)}) collective-permute-start(bf16[128,2048]{1,0:T(8,128)(2,1)} %get-tuple-element.11), channel_id=1, source_target_pairs={{0,3},{1,0},{2,1},{3,2},{4,7},{5,4},{6,5},{7,6},{8,11},{9,8},{10,9... | collective-permute-start | bytes 1572872 | tf_op jit(solution)/shard_map/ppermute | solution.py:147
  27.5 59.3 %collective-permute-start.5 = (bf16[128,2048]{1,0:T(8,128)(2,1)}, bf16[128,2048]{1,0:T(8,128)(2,1)S(1)}, u32[]{:S(2)}, u32[]{:S(2)}) collective-permute-start(bf16[128,2048]{1,0:T(8,128)(2,1)} %get-tuple-element.14), channel_id=1, source_target_pairs={{0,2},{1,3},{2,0},{3,1},{4,6},{5,7},{6,4},{7,5},{8,10},{9,11},{10,... | collective-permute-start | bytes 1572872 | tf_op jit(solution)/shard_map/ppermute | solution.py:147
  28.6 40.0 %collective-permute-start.3 = (bf16[128,2048]{1,0:T(8,128)(2,1)}, bf16[128,2048]{1,0:T(8,128)(2,1)}, u32[]{:S(2)}, u32[]{:S(2)}) collective-permute-start(bf16[128,2048]{1,0:T(8,128)(2,1)} %get-tuple-element.12), channel_id=1, source_target_pairs={{0,1},{1,2},{2,3},{3,0},{4,5},{5,6},{6,7},{7,4},{8,9},{9,10},{10,1... | collective-permute-start | bytes 1572872 | tf_op jit(solution)/shard_map/ppermute | solution.py:147
  29.7 36.4 %copy-start.7 = (s32[128]{0:T(128)}, s32[128]{0:T(128)S(1)}, u32[]{:S(2)}) copy-start(s32[128]{0:T(128)S(1)} %get-tuple-element.8) | copy-start | bytes 1540
  29.7 36.4 %copy-start.8 = (s32[128]{0:T(128)}, s32[128]{0:T(128)S(1)}, u32[]{:S(2)}) copy-start(s32[128]{0:T(128)S(1)} %get-tuple-element.5) | copy-start | bytes 1540
  29.7 36.4 %copy-start.9 = (s32[128]{0:T(128)}, s32[128]{0:T(128)S(1)}, u32[]{:S(2)}) copy-start(s32[128]{0:T(128)S(1)} %get-tuple-element.7) | copy-start | bytes 1540
  29.7 36.4 %copy-start.10 = (s32[128]{0:T(128)}, s32[128]{0:T(128)S(1)}, u32[]{:S(2)}) copy-start(s32[128]{0:T(128)S(1)} %get-tuple-element.6) | copy-start | bytes 1540
  82.5 53.7 %collective-permute-start.4 = (bf16[128,2048]{1,0:T(8,128)(2,1)}, bf16[128,2048]{1,0:T(8,128)(2,1)S(1)}, u32[]{:S(2)}, u32[]{:S(2)}) collective-permute-start(bf16[128,2048]{1,0:T(8,128)(2,1)} %shard_map.47), channel_id=1, source_target_pairs={{0,3},{1,0},{2,1},{3,2},{4,7},{5,4},{6,5},{7,6},{8,11},{9,8},{10,9... | collective-permute-start | bytes 1572872 | tf_op jit(solution)/shard_map/ppermute | solution.py:151
  86.7 0.8 copy-start.5
  101.4 36.1 %collective-permute-start.6 = (bf16[128,2048]{1,0:T(8,128)(2,1)}, bf16[128,2048]{1,0:T(8,128)(2,1)S(1)}, u32[]{:S(2)}, u32[]{:S(2)}) collective-permute-start(bf16[128,2048]{1,0:T(8,128)(2,1)} %shard_map.48), channel_id=1, source_target_pairs={{0,2},{1,3},{2,0},{3,1},{4,6},{5,7},{6,4},{7,5},{8,10},{9,11},{10,... | collective-permute-start | bytes 1572872 | tf_op jit(solution)/shard_map/ppermute | solution.py:151
  105.1 0.8 copy-start.4
  119.7 17.8 %collective-permute-start.8 = (bf16[128,2048]{1,0:T(8,128)(2,1)}, bf16[128,2048]{1,0:T(8,128)(2,1)S(1)}, u32[]{:S(2)}, u32[]{:S(2)}) collective-permute-start(bf16[128,2048]{1,0:T(8,128)(2,1)} %shard_map.49), channel_id=1, source_target_pairs={{0,1},{1,2},{2,3},{3,0},{4,5},{5,6},{6,7},{7,4},{8,9},{9,10},{10,1... | collective-permute-start | bytes 1572872 | tf_op jit(solution)/shard_map/ppermute | solution.py:151
  135.1 1.0 copy-start.1
  137.6 1.3 copy-start
Sparse Core Ops, SparseCore 0:
  23.1 39.0 all-gather.1

commit v2 on v1

--- a/solution.py
+++ b/solution.py
@@ -11,6 +11,7 @@
 HEAD_DIM = 128
 KEY_ROWS = 512
 DOC_MOST = 3584
+WINDOW_BLOCKS = -(-DOC_MOST // KEY_ROWS) + 1
 NEG_START = -1e30
 
 
@@ -75,8 +76,7 @@
 def attend(q_tile, q_off, keys, values_t, doc_ids, groups, heads_per):
     tokens = doc_ids.shape[0]
     q_rows = q_tile.shape[0]
-    blocks = tokens // KEY_ROWS
-    steps = min(blocks, -(-DOC_MOST // KEY_ROWS) + 1)
+    steps = keys.shape[0]
     query_doc = lax.dynamic_slice_in_dim(doc_ids, q_off, q_rows)
     query_start = jnp.sum((doc_ids[None, :] < query_doc[:, None]).astype(jnp.int32), axis=1).reshape(1, q_rows)
     meta = jnp.stack([query_start[0, 0] // KEY_ROWS, (q_off + q_rows - 1) // KEY_ROWS, q_off]).astype(jnp.int32)
@@ -85,7 +85,7 @@
     heads = groups * heads_per
 
     def key_index(j, meta, docs):
-        return jnp.minimum(meta[0] + j, meta[1])
+        return jnp.minimum(meta[0] + j, meta[1]) - meta[1] + steps - 1
 
     kernel = functools.partial(
         flash_kernel, heads_per=heads_per, groups=groups, q_rows=q_rows, steps=steps,
@@ -99,8 +99,8 @@
             grid=(steps,),
             in_specs=[
                 pl.BlockSpec((q_rows, width), lambda j, meta, docs: (0, 0)),
-                pl.BlockSpec((KEY_ROWS, kv_width), lambda j, meta, docs: (key_index(j, meta, docs), 0)),
-                pl.BlockSpec((kv_width, KEY_ROWS), lambda j, meta, docs: (0, key_index(j, meta, docs))),
+                pl.BlockSpec((None, KEY_ROWS, kv_width), lambda j, meta, docs: (key_index(j, meta, docs), 0, 0)),
+                pl.BlockSpec((None, kv_width, KEY_ROWS), lambda j, meta, docs: (key_index(j, meta, docs), 0, 0)),
                 pl.BlockSpec((1, q_rows), lambda j, meta, docs: (0, 0)),
             ],
             out_specs=pl.BlockSpec((q_rows, width), lambda j, meta, docs: (0, 0)),
@@ -127,8 +127,15 @@
         if t:
             piece = lax.ppermute(piece, "head", [(i, (i + t) % head_count) for i in range(head_count)])
         local = lax.dynamic_update_slice_in_dim(local, piece, ((head - t) % head_count) * sub, axis=0)
-    whole = lax.all_gather(local, "seq", axis=0, tiled=True)
-    return whole[:, 0, :], whole[:, 1, :].T
+    seq_count = lax.axis_size("seq")
+    window = min(seq_count, WINDOW_BLOCKS)
+    slots = [local]
+    for d in range(1, window):
+        slots.append(lax.ppermute(local, "seq", [(i, i + d) for i in range(seq_count - d)]))
+    slots = slots[::-1]
+    keys = jnp.stack([slot[:, 0, :] for slot in slots])
+    values_t = jnp.stack([slot[:, 1, :].T for slot in slots])
+    return keys, values_t
 
 
 def body(query_rows, key_rows, value_rows, doc_ids):

time: 147 us -> 154 us (1.048)
  the two profiles are of different devices: /device:TPU:5 before, /device:TPU:4 now
where the time goes in v2:
time: 154 us; the launch traced here: 156 us
  Pallas kernels  49 us (32%)
  waiting for transfers between devices  44.1 us (29%)
  starting transfers between devices  40.6 us (26%)
  local copies, waits for them, and re-layouts  17.6 us (11%)
  other arithmetic  3.45 us (2%)
    pallas_call x4, Pallas kernels, attend(): pl.pallas_call(kernel, out_shape=jax.ShapeDtypeStruct((q_rows, width), jn...  49 us
    ppermute x7, waiting for transfers between devices, gather_kv(): lax.ppermute(local, 'seq', [(i, i + d) for i in range(seq_count - d)])  29.9 us
    ppermute x7, starting transfers between devices, gather_kv(): lax.ppermute(local, 'seq', [(i, i + d) for i in range(seq_count - d)])  26.2 us
    unnamed x42, local copies, waits for them, and re-layouts  10.9 us
    ppermute x3, waiting for transfers between devices, gather_kv(): lax.ppermute(piece, 'head', [(i, (i + t) % head_count) for i in range(hea...  7.26 us
    ppermute x3, waiting for transfers between devices, body(): lax.ppermute(out_tile, 'head', [(i, (i - t) % head_count) for i in range(...  6.88 us
    ppermute x3, starting transfers between devices, gather_kv(): lax.ppermute(piece, 'head', [(i, (i + t) % head_count) for i in range(hea...  5.57 us
    ppermute x3, starting transfers between devices, body(): lax.ppermute(piece, 'head', [(i, (i + t) % head_count) for i in range(hea...  4.74 us
  transfers between devices with their start and end apart: 16, of which 5 were waited for; matrix products, arithmetic and copies ran while one was open for 9% of the time, Pallas kernels for 31%

profile of v2, /device:TPU:4, one launch (start us, length us, event | category | flops | bytes accessed | tf_op | source)
XLA Modules:
  0.0 155.9 jit_solution(9997512560730653781)
XLA Ops:
  0.0 1.3 copy.11
  1.3 1.1 copy.12
  2.5 0.1 fusion.16
  2.6 1.6 %collective-permute-start = (bf16[128,2,256]{0,2,1:T(8,128)(2,1)S(1)}, bf16[128,2,256]{0,2,1:T(8,128)(2,1)S(1)}, u32[]{:S(2)}, u32[]{:S(2)}) collective-permute-start(bf16[128,2,256]{0,2,1:T(8,128)(2,1)S(1)} %get-tuple-element.15), channel_id=1, source_target_pairs={{0,1},{1,2},{2,3},{3,0},{4,5},{5,6},{6,7},{7,4},{8,9},{9,10},{10,1... | collective-permute-start | bytes 393224 | tf_op jit(solution)/shard_map/ppermute | solution.py:128
  4.2 2.6 %collective-permute-start.1 = (bf16[128,2,256]{0,2,1:T(8,128)(2,1)S(1)}, bf16[128,2,256]{0,2,1:T(8,128)(2,1)S(1)}, u32[]{:S(2)}, u32[]{:S(2)}) collective-permute-start(bf16[128,2,256]{0,2,1:T(8,128)(2,1)S(1)} %get-tuple-element.16), channel_id=1, source_target_pairs={{0,2},{1,3},{2,0},{3,1},{4,6},{5,7},{6,4},{7,5},{8,10},{9,11},{10,... | collective-permute-start | bytes 393224 | tf_op jit(solution)/shard_map/ppermute | solution.py:128
  6.8 1.3 collective-permute-start.2
  8.1 2.8 %collective-permute-done = bf16[128,2,256]{0,2,1:T(8,128)(2,1)S(1)} collective-permute-done((bf16[128,2,256]{0,2,1:T(8,128)(2,1)S(1)}, bf16[128,2,256]{0,2,1:T(8,128)(2,1)S(1)}, u32[]{:S(2)}, u32[]{:S(2)}) %collective-permute-start) | collective-permute-done | bytes 131104 | tf_op jit(solution)/shard_map/ppermute | solution.py:128
  10.9 4.5 %collective-permute-done.1 = bf16[128,2,256]{0,2,1:T(8,128)(2,1)S(1)} collective-permute-done((bf16[128,2,256]{0,2,1:T(8,128)(2,1)S(1)}, bf16[128,2,256]{0,2,1:T(8,128)(2,1)S(1)}, u32[]{:S(2)}, u32[]{:S(2)}) %collective-permute-start.1) | collective-permute-done | bytes 131104 | tf_op jit(solution)/shard_map/ppermute | solution.py:128
  15.5 0.0 copy-start.8
  15.5 1.5 collective-permute-start.3
  17.0 1.3 constant_dynamic-slice_fusion
  18.3 4.3 %collective-permute-start.14 = (bf16[128,2048]{1,0:T(8,128)(2,1)}, bf16[128,2048]{1,0:T(8,128)(2,1)S(1)}, u32[]{:S(2)}, u32[]{:S(2)}) collective-permute-start(bf16[128,2048]{1,0:T(8,128)(2,1)} %get-tuple-element.9), channel_id=1, source_target_pairs={{0,3},{1,0},{2,1},{3,2},{4,7},{5,4},{6,5},{7,6},{8,11},{9,8},{10,9... | collective-permute-start | bytes 1572872 | tf_op jit(solution)/shard_map/ppermute | solution.py:154
  22.7 0.3 collective-permute-start.12
  23.0 0.1 fusion.21
  23.1 0.7 collective-permute-start.4
  23.8 1.0 convert_reduce_fusion
  25.0 0.7 collective-permute-start.5
  25.7 0.6 pad_add_fusion.1.meta_ref
  26.9 1.3 collective-permute-start.6
  28.2 1.0 fusion.15
  29.1 11.1 %collective-permute-start.7 = (bf16[512,2,256]{0,2,1:T(8,128)(2,1)S(1)}, bf16[512,2,256]{0,2,1:T(8,128)(2,1)S(1)}, u32[]{:S(2)}, u32[]{:S(2)}) collective-permute-start(bf16[512,2,256]{0,2,1:T(8,128)(2,1)S(1)} %constant_dynamic-update-slice_fusion.4), channel_id=1, source_target_pairs={{0,12},{4,16},{8,20},{12,24},{16,28},{1,13},{5,17},{9,21},{13,25},... | collective-permute-start | bytes 1572872 | tf_op jit(solution)/shard_map/ppermute | solution.py:134
  40.3 9.0 %collective-permute-start.8 = (bf16[512,2,256]{0,2,1:T(8,128)(2,1)S(1)}, bf16[512,2,256]{0,2,1:T(8,128)(2,1)S(1)}, u32[]{:S(2)}, u32[]{:S(2)}) collective-permute-start(bf16[512,2,256]{0,2,1:T(8,128)(2,1)S(1)} %constant_dynamic-update-slice_fusion.4), channel_id=1, source_target_pairs={{0,8},{4,12},{8,16},{12,20},{16,24},{20,28},{1,9},{5,13},{9,17},{1... | collective-permute-start | bytes 1572872 | tf_op jit(solution)/shard_map/ppermute | solution.py:134
  49.3 20.6 %collective-permute-done.6 = bf16[512,2,256]{0,2,1:T(8,128)(2,1)S(1)} collective-permute-done((bf16[512,2,256]{0,2,1:T(8,128)(2,1)S(1)}, bf16[512,2,256]{0,2,1:T(8,128)(2,1)S(1)}, u32[]{:S(2)}, u32[]{:S(2)}) %collective-permute-start.6) | collective-permute-done | bytes 524320 | tf_op jit(solution)/shard_map/ppermute | solution.py:134
  69.9 1.9 %collective-permute-start.9 = (bf16[512,2,256]{0,2,1:T(8,128)(2,1)S(1)}, bf16[512,2,256]{0,2,1:T(8,128)(2,1)S(1)}, u32[]{:S(2)}, u32[]{:S(2)}) collective-permute-start(bf16[512,2,256]{0,2,1:T(8,128)(2,1)S(1)} %constant_dynamic-update-slice_fusion.4), channel_id=1, source_target_pairs={{0,4},{4,8},{8,12},{12,16},{16,20},{20,24},{24,28},{1,5},{5,9},{9,... | collective-permute-start | bytes 1572872 | tf_op jit(solution)/shard_map/ppermute | solution.py:134
  71.9 0.1 collective-permute-start.10
  72.0 9.3 %collective-permute-done.9 = bf16[512,2,256]{0,2,1:T(8,128)(2,1)S(1)} collective-permute-done((bf16[512,2,256]{0,2,1:T(8,128)(2,1)S(1)}, bf16[512,2,256]{0,2,1:T(8,128)(2,1)S(1)}, u32[]{:S(2)}, u32[]{:S(2)}) %collective-permute-start.9) | collective-permute-done | bytes 524320 | tf_op jit(solution)/shard_map/ppermute | solution.py:134
  81.4 1.2 fusion.7
  82.6 1.0 fusion.6
  83.6 1.0 fusion.5
  84.7 3.9 %copy.13.k_ref = bf16[8,512,256]{2,1,0:T(8,128)(2,1)} copy(bf16[8,512,256]{1,2,0:T(8,128)(2,1)} %copy-done.1) | data formatting | bytes 4194304 | tf_op jit(solution)/shard_map/stack | solution.py:136
  88.6 0.0 copy-start
  88.7 1.3 copy-done
  90.0 12.2 %shard_map.47 = bf16[128,2048]{1,0:T(8,128)(2,1)} custom-call(s32[3]{0:T(128)} %pad_add_fusion.1.meta_ref, s32[4096]{0:T(1024)} %doc_ref.7, bf16[128,2048]{1,0:T(8,128)(2,1)} %collective-permute-done.10.q_ref, bf16[8,512,256]{2,1,0:T(8,128)(2,1)} %copy.13.k_ref, bf16[8,256,512]{2,1,0:T(8,128)(2,1)} %copy-done, s32[1,128]{1,0:T(1,128)} %bitcast.143), custom_call_target="tpu_custom_call" | custom-call | tf_op jit(solution)/shard_map/pallas_call | solution.py:94
  102.2 0.9 collective-permute-start.11
  103.1 0.6 pad_add_fusion.3.meta_ref
  103.7 0.6 pad_add_fusion.2.meta_ref
  104.3 12.2 %shard_map.48 = bf16[128,2048]{1,0:T(8,128)(2,1)} custom-call(s32[3]{0:T(128)} %pad_add_fusion.2.meta_ref, s32[4096]{0:T(1024)} %doc_ref.7, bf16[128,2048]{1,0:T(8,128)(2,1)} %collective-permute-done.12.q_ref, bf16[8,512,256]{2,1,0:T(8,128)(2,1)} %copy.13.k_ref, bf16[8,256,512]{2,1,0:T(8,128)(2,1)} %copy-done, s32[1,128]{1,0:T(1,128)} %bitcast.138), custom_call_target="tpu_custom_call" | custom-call | tf_op jit(solution)/shard_map/pallas_call | solution.py:94
  116.6 1.2 collective-permute-start.13
  117.8 0.6 pad_add_fusion.meta_ref
  118.3 0.8 copy-done.5
  119.1 12.2 %shard_map.49 = bf16[128,2048]{1,0:T(8,128)(2,1)} custom-call(s32[3]{0:T(128)} %pad_add_fusion.3.meta_ref, s32[4096]{0:T(1024)} %doc_ref.7, bf16[128,2048]{1,0:T(8,128)(2,1)} %copy-done.5, bf16[8,512,256]{2,1,0:T(8,128)(2,1)} %copy.13.k_ref, bf16[8,256,512]{2,1,0:T(8,128)(2,1)} %copy-done, s32[1,128]{1,0:T(1,128)} %bitcast.133), custom_call_target="tpu_custom_call" | custom-call | tf_op jit(solution)/shard_map/pallas_call | solution.py:94
  131.4 2.0 %collective-permute-start.15 = (bf16[128,2048]{1,0:T(8,128)(2,1)}, bf16[128,2048]{1,0:T(8,128)(2,1)S(1)}, u32[]{:S(2)}, u32[]{:S(2)}) collective-permute-start(bf16[128,2048]{1,0:T(8,128)(2,1)} %shard_map.49), channel_id=1, source_target_pairs={{0,1},{1,2},{2,3},{3,0},{4,5},{5,6},{6,7},{7,4},{8,9},{9,10},{10,1... | collective-permute-start | bytes 1572872 | tf_op jit(solution)/shard_map/ppermute | solution.py:158
  133.4 12.2 %shard_map.46 = bf16[128,2048]{1,0:T(8,128)(2,1)} custom-call(s32[3]{0:T(128)} %pad_add_fusion.meta_ref, s32[4096]{0:T(1024)} %doc_ref.7, bf16[128,2048]{1,0:T(8,128)(2,1)} %get-tuple-element.11.q_ref, bf16[8,512,256]{2,1,0:T(8,128)(2,1)} %copy.13.k_ref, bf16[8,256,512]{2,1,0:T(8,128)(2,1)} %copy-done, s32[1,128]{1,0:T(1,128)} %bitcast.128), custom_call_target="tpu_custom_call" | custom-call | tf_op jit(solution)/shard_map/pallas_call | solution.py:94
  145.6 0.2 broadcast_in_dim.4
  145.8 0.8 copy-done.3
  146.8 6.9 %collective-permute-done.13 = bf16[128,2048]{1,0:T(8,128)(2,1)S(1)} collective-permute-done((bf16[128,2048]{1,0:T(8,128)(2,1)}, bf16[128,2048]{1,0:T(8,128)(2,1)S(1)}, u32[]{:S(2)}, u32[]{:S(2)}) %collective-permute-start.13) | collective-permute-done | bytes 524320 | tf_op jit(solution)/shard_map/ppermute | solution.py:158
  153.7 1.3 copy-done.2
  155.0 0.8 constant_dynamic-update-slice_fusion
  (50 shorter events, 0.6 us)
Async XLA Ops:
  0.0 17.0 %copy-start.4 = (bf16[128,8192]{1,0:T(8,128)(2,1)S(1)}, bf16[128,8192]{1,0:T(8,128)(2,1)}, u32[]{:S(2)}) copy-start(bf16[128,8192]{1,0:T(8,128)(2,1)} %param.4) | copy-start | bytes 6291460
  2.6 8.3 %collective-permute-start = (bf16[128,2,256]{0,2,1:T(8,128)(2,1)S(1)}, bf16[128,2,256]{0,2,1:T(8,128)(2,1)S(1)}, u32[]{:S(2)}, u32[]{:S(2)}) collective-permute-start(bf16[128,2,256]{0,2,1:T(8,128)(2,1)S(1)} %get-tuple-element.15), channel_id=1, source_target_pairs={{0,1},{1,2},{2,3},{3,0},{4,5},{5,6},{6,7},{7,4},{8,9},{9,10},{10,1... | collective-permute-start | bytes 393224 | tf_op jit(solution)/shard_map/ppermute | solution.py:128
  4.2 11.2 %collective-permute-start.1 = (bf16[128,2,256]{0,2,1:T(8,128)(2,1)S(1)}, bf16[128,2,256]{0,2,1:T(8,128)(2,1)S(1)}, u32[]{:S(2)}, u32[]{:S(2)}) collective-permute-start(bf16[128,2,256]{0,2,1:T(8,128)(2,1)S(1)} %get-tuple-element.16), channel_id=1, source_target_pairs={{0,2},{1,3},{2,0},{3,1},{4,6},{5,7},{6,4},{7,5},{8,10},{9,11},{10,... | collective-permute-start | bytes 393224 | tf_op jit(solution)/shard_map/ppermute | solution.py:128
  6.8 8.7 %collective-permute-start.2 = (bf16[128,2,256]{0,2,1:T(8,128)(2,1)S(1)}, bf16[128,2,256]{0,2,1:T(8,128)(2,1)S(1)}, u32[]{:S(2)}, u32[]{:S(2)}) collective-permute-start(bf16[128,2,256]{0,2,1:T(8,128)(2,1)S(1)} %get-tuple-element.13), channel_id=1, source_target_pairs={{0,3},{1,0},{2,1},{3,2},{4,7},{5,4},{6,5},{7,6},{8,11},{9,8},{10,9... | collective-permute-start | bytes 393224 | tf_op jit(solution)/shard_map/ppermute | solution.py:128
  15.5 7.5 %copy-start.8 = (s32[4096]{0:T(1024)S(1)}, s32[4096]{0:T(1024)}, u32[]{:S(2)}) copy-start(s32[4096]{0:T(1024)} %doc_ref.7) | copy-start | bytes 49156
  15.5 11.3 %collective-permute-start.3 = (bf16[512,2,256]{0,2,1:T(8,128)(2,1)S(1)}, bf16[512,2,256]{0,2,1:T(8,128)(2,1)}, u32[]{:S(2)}, u32[]{:S(2)}) collective-permute-start(bf16[512,2,256]{0,2,1:T(8,128)(2,1)S(1)} %constant_dynamic-update-slice_fusion.4), channel_id=1, source_target_pairs={{0,28},{1,29},{2,30},{3,31}} | collective-permute-start | bytes 1572872 | tf_op jit(solution)/shard_map/ppermute | solution.py:134
  18.3 100.0 %collective-permute-start.14 = (bf16[128,2048]{1,0:T(8,128)(2,1)}, bf16[128,2048]{1,0:T(8,128)(2,1)S(1)}, u32[]{:S(2)}, u32[]{:S(2)}) collective-permute-start(bf16[128,2048]{1,0:T(8,128)(2,1)} %get-tuple-element.9), channel_id=1, source_target_pairs={{0,3},{1,0},{2,1},{3,2},{4,7},{5,4},{6,5},{7,6},{8,11},{9,8},{10,9... | collective-permute-start | bytes 1572872 | tf_op jit(solution)/shard_map/ppermute | solution.py:154
  22.7 81.6 %collective-permute-start.12 = (bf16[128,2048]{1,0:T(8,128)(2,1)}, bf16[128,2048]{1,0:T(8,128)(2,1)}, u32[]{:S(2)}, u32[]{:S(2)}) collective-permute-start(bf16[128,2048]{1,0:T(8,128)(2,1)} %get-tuple-element.12), channel_id=1, source_target_pairs={{0,2},{1,3},{2,0},{3,1},{4,6},{5,7},{6,4},{7,5},{8,10},{9,11},{10,... | collective-permute-start | bytes 1572872 | tf_op jit(solution)/shard_map/ppermute | solution.py:154
  23.1 6.0 %collective-permute-start.4 = (bf16[512,2,256]{0,2,1:T(8,128)(2,1)S(1)}, bf16[512,2,256]{0,2,1:T(8,128)(2,1)S(1)}, u32[]{:S(2)}, u32[]{:S(2)}) collective-permute-start(bf16[512,2,256]{0,2,1:T(8,128)(2,1)S(1)} %constant_dynamic-update-slice_fusion.4), channel_id=1, source_target_pairs={{0,24},{4,28},{1,25},{5,29},{2,26},{6,30},{3,27},{7,31}} | collective-permute-start | bytes 1572872 | tf_op jit(solution)/shard_map/ppermute | solution.py:134
  24.8 56.6 %copy-start.9 = (s32[128]{0:T(128)}, s32[128]{0:T(128)S(1)}, u32[]{:S(2)}) copy-start(s32[128]{0:T(128)S(1)} %get-tuple-element.8) | copy-start | bytes 1540
  24.8 56.6 %copy-start.10 = (s32[128]{0:T(128)}, s32[128]{0:T(128)S(1)}, u32[]{:S(2)}) copy-start(s32[128]{0:T(128)S(1)} %get-tuple-element.5) | copy-start | bytes 1540
  24.8 56.6 %copy-start.11 = (s32[128]{0:T(128)}, s32[128]{0:T(128)S(1)}, u32[]{:S(2)}) copy-start(s32[128]{0:T(128)S(1)} %get-tuple-element.7) | copy-start | bytes 1540
  24.8 56.6 %copy-start.12 = (s32[128]{0:T(128)}, s32[128]{0:T(128)S(1)}, u32[]{:S(2)}) copy-start(s32[128]{0:T(128)S(1)} %get-tuple-element.6) | copy-start | bytes 1540
  25.0 15.2 %collective-permute-start.5 = (bf16[512,2,256]{0,2,1:T(8,128)(2,1)S(1)}, bf16[512,2,256]{0,2,1:T(8,128)(2,1)S(1)}, u32[]{:S(2)}, u32[]{:S(2)}) collective-permute-start(bf16[512,2,256]{0,2,1:T(8,128)(2,1)S(1)} %constant_dynamic-update-slice_fusion.4), channel_id=1, source_target_pairs={{0,20},{4,24},{8,28},{1,21},{5,25},{9,29},{2,22},{6,26},{10,30},{3... | collective-permute-start | bytes 1572872 | tf_op jit(solution)/shard_map/ppermute | solution.py:134
  26.9 43.1 %collective-permute-start.6 = (bf16[512,2,256]{0,2,1:T(8,128)(2,1)S(1)}, bf16[512,2,256]{0,2,1:T(8,128)(2,1)S(1)}, u32[]{:S(2)}, u32[]{:S(2)}) collective-permute-start(bf16[512,2,256]{0,2,1:T(8,128)(2,1)S(1)} %constant_dynamic-update-slice_fusion.4), channel_id=1, source_target_pairs={{0,16},{4,20},{8,24},{12,28},{1,17},{5,21},{9,25},{13,29},{2,18},{... | collective-permute-start | bytes 1572872 | tf_op jit(solution)/shard_map/ppermute | solution.py:134
  29.1 52.2 %copy-start.6 = (bf16[512,2,256]{0,2,1:T(8,128)(2,1)}, bf16[512,2,256]{0,2,1:T(8,128)(2,1)S(1)}, u32[]{:S(2)}) copy-start(bf16[512,2,256]{0,2,1:T(8,128)(2,1)S(1)} %collective-permute-done.4) | copy-start | bytes 1572868
  29.1 42.7 %collective-permute-start.7 = (bf16[512,2,256]{0,2,1:T(8,128)(2,1)S(1)}, bf16[512,2,256]{0,2,1:T(8,128)(2,1)S(1)}, u32[]{:S(2)}, u32[]{:S(2)}) collective-permute-start(bf16[512,2,256]{0,2,1:T(8,128)(2,1)S(1)} %constant_dynamic-update-slice_fusion.4), channel_id=1, source_target_pairs={{0,12},{4,16},{8,20},{12,24},{16,28},{1,13},{5,17},{9,21},{13,25},... | collective-permute-start | bytes 1572872 | tf_op jit(solution)/shard_map/ppermute | solution.py:134
  40.2 41.1 %copy-start.7 = (bf16[512,2,256]{0,2,1:T(8,128)(2,1)}, bf16[512,2,256]{0,2,1:T(8,128)(2,1)S(1)}, u32[]{:S(2)}) copy-start(bf16[512,2,256]{0,2,1:T(8,128)(2,1)S(1)} %collective-permute-done.5) | copy-start | bytes 1572868
  40.3 31.7 %collective-permute-start.8 = (bf16[512,2,256]{0,2,1:T(8,128)(2,1)S(1)}, bf16[512,2,256]{0,2,1:T(8,128)(2,1)S(1)}, u32[]{:S(2)}, u32[]{:S(2)}) collective-permute-start(bf16[512,2,256]{0,2,1:T(8,128)(2,1)S(1)} %constant_dynamic-update-slice_fusion.4), channel_id=1, source_target_pairs={{0,8},{4,12},{8,16},{12,20},{16,24},{20,28},{1,9},{5,13},{9,17},{1... | collective-permute-start | bytes 1572872 | tf_op jit(solution)/shard_map/ppermute | solution.py:134
  69.9 11.4 %collective-permute-start.9 = (bf16[512,2,256]{0,2,1:T(8,128)(2,1)S(1)}, bf16[512,2,256]{0,2,1:T(8,128)(2,1)S(1)}, u32[]{:S(2)}, u32[]{:S(2)}) collective-permute-start(bf16[512,2,256]{0,2,1:T(8,128)(2,1)S(1)} %constant_dynamic-update-slice_fusion.4), channel_id=1, source_target_pairs={{0,4},{4,8},{8,12},{12,16},{16,20},{20,24},{24,28},{1,5},{5,9},{9,... | collective-permute-start | bytes 1572872 | tf_op jit(solution)/shard_map/ppermute | solution.py:134
  71.9 16.8 %collective-permute-start.10 = (bf16[128,2048]{1,0:T(8,128)(2,1)}, bf16[128,2048]{1,0:T(8,128)(2,1)}, u32[]{:S(2)}, u32[]{:S(2)}) collective-permute-start(bf16[128,2048]{1,0:T(8,128)(2,1)} %get-tuple-element.10), channel_id=1, source_target_pairs={{0,1},{1,2},{2,3},{3,0},{4,5},{5,6},{6,7},{7,4},{8,9},{9,10},{10,1... | collective-permute-start | bytes 1572872 | tf_op jit(solution)/shard_map/ppermute | solution.py:154
  81.4 3.2 %copy-start.1 = (bf16[8,512,256]{1,2,0:T(8,128)(2,1)}, bf16[8,512,256]{1,2,0:T(8,128)(2,1)S(1)}, u32[]{:S(2)}) copy-start(bf16[8,512,256]{1,2,0:T(8,128)(2,1)S(1)} %fusion.8) | copy-start | bytes 6291460
  88.6 1.3 copy-start
  102.2 44.5 %collective-permute-start.11 = (bf16[128,2048]{1,0:T(8,128)(2,1)}, bf16[128,2048]{1,0:T(8,128)(2,1)S(1)}, u32[]{:S(2)}, u32[]{:S(2)}) collective-permute-start(bf16[128,2048]{1,0:T(8,128)(2,1)} %shard_map.47), channel_id=1, source_target_pairs={{0,3},{1,0},{2,1},{3,2},{4,7},{5,4},{6,5},{7,6},{8,11},{9,8},{10,9... | collective-permute-start | bytes 1572872 | tf_op jit(solution)/shard_map/ppermute | solution.py:158
  116.6 37.1 %collective-permute-start.13 = (bf16[128,2048]{1,0:T(8,128)(2,1)}, bf16[128,2048]{1,0:T(8,128)(2,1)S(1)}, u32[]{:S(2)}, u32[]{:S(2)}) collective-permute-start(bf16[128,2048]{1,0:T(8,128)(2,1)} %shard_map.48), channel_id=1, source_target_pairs={{0,2},{1,3},{2,0},{3,1},{4,6},{5,7},{6,4},{7,5},{8,10},{9,11},{10,... | collective-permute-start | bytes 1572872 | tf_op jit(solution)/shard_map/ppermute | solution.py:158
  118.3 0.8 copy-start.5
  131.4 22.4 %collective-permute-start.15 = (bf16[128,2048]{1,0:T(8,128)(2,1)}, bf16[128,2048]{1,0:T(8,128)(2,1)S(1)}, u32[]{:S(2)}, u32[]{:S(2)}) collective-permute-start(bf16[128,2048]{1,0:T(8,128)(2,1)} %shard_map.49), channel_id=1, source_target_pairs={{0,1},{1,2},{2,3},{3,0},{4,5},{5,6},{6,7},{7,4},{8,9},{9,10},{10,1... | collective-permute-start | bytes 1572872 | tf_op jit(solution)/shard_map/ppermute | solution.py:158
  145.6 1.0 copy-start.3
  153.7 1.3 copy-start.2

commit v3 on v1

--- a/solution.py
+++ b/solution.py
@@ -99,8 +99,8 @@
             grid=(steps,),
             in_specs=[
                 pl.BlockSpec((q_rows, width), lambda j, meta, docs: (0, 0)),
-                pl.BlockSpec((KEY_ROWS, kv_width), lambda j, meta, docs: (key_index(j, meta, docs), 0)),
-                pl.BlockSpec((kv_width, KEY_ROWS), lambda j, meta, docs: (0, key_index(j, meta, docs))),
+                pl.BlockSpec((None, KEY_ROWS, kv_width), lambda j, meta, docs: (key_index(j, meta, docs), 0, 0)),
+                pl.BlockSpec((None, kv_width, KEY_ROWS), lambda j, meta, docs: (key_index(j, meta, docs), 0, 0)),
                 pl.BlockSpec((1, q_rows), lambda j, meta, docs: (0, 0)),
             ],
             out_specs=pl.BlockSpec((q_rows, width), lambda j, meta, docs: (0, 0)),
@@ -127,8 +127,9 @@
         if t:
             piece = lax.ppermute(piece, "head", [(i, (i + t) % head_count) for i in range(head_count)])
         local = lax.dynamic_update_slice_in_dim(local, piece, ((head - t) % head_count) * sub, axis=0)
-    whole = lax.all_gather(local, "seq", axis=0, tiled=True)
-    return whole[:, 0, :], whole[:, 1, :].T
+    keys = lax.all_gather(local[:, 0, :], "seq", axis=0)
+    values_t = lax.all_gather(local[:, 1, :].T, "seq", axis=0)
+    return keys, values_t
 
 
 def body(query_rows, key_rows, value_rows, doc_ids):

time: 147 us -> 153 us (1.041)
  the two profiles are of different devices: /device:TPU:5 before, /device:TPU:6 now
where the time goes in v3:
time: 153 us; the launch traced here: 150 us
  waiting for transfers between devices  67.8 us (44%)
  Pallas kernels  36.5 us (24%)
  starting transfers between devices  15 us (10%)
  between operations  14.4 us (9%)
  local copies, waits for them, and re-layouts  11.7 us (8%)
  other arithmetic  4.53 us (3%)
    pallas_call x4, Pallas kernels, attend(): pl.pallas_call(kernel, out_shape=jax.ShapeDtypeStruct((q_rows, width), jn...  36.5 us
    all_gather x1, waiting for transfers between devices, gather_kv(): values_t = lax.all_gather(local[:, 1, :].T, 'seq', axis=0)  25.7 us
    all_gather x1, waiting for transfers between devices, gather_kv(): keys = lax.all_gather(local[:, 0, :], 'seq', axis=0)  20.1 us
    ppermute x3, waiting for transfers between devices, body(): lax.ppermute(out_tile, 'head', [(i, (i - t) % head_count) for i in range(...  14.5 us
    ppermute x3, waiting for transfers between devices, gather_kv(): lax.ppermute(piece, 'head', [(i, (i + t) % head_count) for i in range(hea...  6.83 us
    ppermute x3, starting transfers between devices, gather_kv(): lax.ppermute(piece, 'head', [(i, (i + t) % head_count) for i in range(hea...  5.57 us
    ppermute x3, starting transfers between devices, body(): lax.ppermute(piece, 'head', [(i, (i + t) % head_count) for i in range(hea...  4.91 us
    ppermute x3, starting transfers between devices, body(): lax.ppermute(out_tile, 'head', [(i, (i - t) % head_count) for i in range(...  4.44 us
  transfers between devices with their start and end apart: 11, of which 5 were waited for; matrix products, arithmetic and copies ran while one was open for 6% of the time, Pallas kernels for 24%

profile of v3, /device:TPU:6, one launch (start us, length us, event | category | flops | bytes accessed | tf_op | source)
XLA Modules:
  0.0 150.0 jit_solution(15843763946282009146)
XLA Ops:
  6.5 1.1 fusion
  7.6 1.6 %collective-permute-start = (bf16[128,2,256]{2,0,1:T(8,128)(2,1)S(1)}, bf16[128,2,256]{2,0,1:T(8,128)(2,1)S(1)}, u32[]{:S(2)}, u32[]{:S(2)}) collective-permute-start(bf16[128,2,256]{2,0,1:T(8,128)(2,1)S(1)} %get-tuple-element.17), channel_id=1, source_target_pairs={{0,1},{1,2},{2,3},{3,0},{4,5},{5,6},{6,7},{7,4},{8,9},{9,10},{10,1... | collective-permute-start | bytes 393224 | tf_op jit(solution)/shard_map/ppermute | solution.py:128
  9.3 2.6 %collective-permute-start.1 = (bf16[128,2,256]{2,0,1:T(8,128)(2,1)S(1)}, bf16[128,2,256]{2,0,1:T(8,128)(2,1)S(1)}, u32[]{:S(2)}, u32[]{:S(2)}) collective-permute-start(bf16[128,2,256]{2,0,1:T(8,128)(2,1)S(1)} %get-tuple-element.18), channel_id=1, source_target_pairs={{0,2},{1,3},{2,0},{3,1},{4,6},{5,7},{6,4},{7,5},{8,10},{9,11},{10,... | collective-permute-start | bytes 393224 | tf_op jit(solution)/shard_map/ppermute | solution.py:128
  11.9 1.3 collective-permute-start.2
  13.2 0.1 copy.10
  13.3 0.0 copy-start.2
  13.5 2.5 %collective-permute-done = bf16[128,2,256]{2,0,1:T(8,128)(2,1)S(1)} collective-permute-done((bf16[128,2,256]{2,0,1:T(8,128)(2,1)S(1)}, bf16[128,2,256]{2,0,1:T(8,128)(2,1)S(1)}, u32[]{:S(2)}, u32[]{:S(2)}) %collective-permute-start) | collective-permute-done | bytes 131104 | tf_op jit(solution)/shard_map/ppermute | solution.py:128
  16.0 0.1 copy.11
  16.1 4.4 %collective-permute-done.1 = bf16[128,2,256]{2,0,1:T(8,128)(2,1)S(1)} collective-permute-done((bf16[128,2,256]{2,0,1:T(8,128)(2,1)S(1)}, bf16[128,2,256]{2,0,1:T(8,128)(2,1)S(1)}, u32[]{:S(2)}, u32[]{:S(2)}) %collective-permute-start.1) | collective-permute-done | bytes 131104 | tf_op jit(solution)/shard_map/ppermute | solution.py:128
  20.5 0.1 copy.12
  20.7 0.0 collective-permute-done.2
  20.7 0.1 copy.13
  20.9 0.8 slice_bitcast_fusion
  21.7 0.0 all-gather.5.cloned.1.call-update
  21.7 0.0 all-gather.7.cloned.1.call-start
  21.8 0.7 all-gather.7.cloned.1.call-update
  22.5 0.0 copy-start.6
  22.5 1.2 constant_dynamic-slice_fusion
  23.7 3.1 %collective-permute-start.3 = (bf16[128,2048]{1,0:T(8,128)(2,1)}, bf16[128,2048]{1,0:T(8,128)(2,1)S(1)}, u32[]{:S(2)}, u32[]{:S(2)}) collective-permute-start(bf16[128,2048]{1,0:T(8,128)(2,1)} %get-tuple-element.10), channel_id=1, source_target_pairs={{0,1},{1,2},{2,3},{3,0},{4,5},{5,6},{6,7},{7,4},{8,9},{9,10},{10,1... | collective-permute-start | bytes 1572872 | tf_op jit(solution)/shard_map/ppermute | solution.py:148
  26.8 1.2 collective-permute-start.7
  28.0 0.6 collective-permute-start.5
  28.6 0.1 fusion.4
  28.7 1.0 convert_reduce_fusion
  30.4 0.6 pad_add_fusion.1.meta_ref
  31.0 20.1 %all-gather.5.cloned.1.call-done = bf16[4096,1,256]{0,2,1:T(8,128)(2,1)} async-done(((bf16[512,1,256]{0,2,1:T(8,128)(2,1)}), bf16[4096,1,256]{0,2,1:T(8,128)(2,1)}) %all-gather.5.cloned.1.call-update) | async-done | bytes 2097168 | tf_op jit(solution)/shard_map/all_gather | solution.py:130
  51.1 4.1 %copy.14 = bf16[4096,1,256]{2,0,1:T(8,128)(2,1)} copy(bf16[4096,1,256]{0,2,1:T(8,128)(2,1)} %all-gather.5.cloned.1.call-done) | data formatting | bytes 4194304 | tf_op jit(solution)/shard_map/all_gather | solution.py:130
  55.2 0.0 collective-permute-done.3.q_ref
  55.2 25.7 %all-gather.7.cloned.1.call-done = bf16[2048,512]{1,0:T(8,128)(2,1)} async-done(((bf16[256,512]{1,0:T(8,128)(2,1)}), bf16[2048,512]{1,0:T(8,128)(2,1)}) %all-gather.7.cloned.1.call-update) | async-done | bytes 2097168 | tf_op jit(solution)/shard_map/all_gather | solution.py:131
  80.9 9.1 %shard_map.47 = bf16[128,2048]{1,0:T(8,128)(2,1)} custom-call(s32[3]{0:T(128)} %pad_add_fusion.1.meta_ref, s32[4096]{0:T(1024)} %doc_ref.7, bf16[128,2048]{1,0:T(8,128)(2,1)} %copy-done.5, bf16[8,512,256]{2,1,0:T(8,128)(2,1)} %bitcast.32, bf16[8,256,512]{2,1,0:T(8,128)(2,1)} %bitcast.36, s32[1,128]{1,0:T(1,128)} %bitcast.61), custom_call_target="tpu_custom_call" | custom-call | tf_op jit(solution)/shard_map/pallas_call | solution.py:94
  90.0 3.3 %collective-permute-start.4 = (bf16[128,2048]{1,0:T(8,128)(2,1)}, bf16[128,2048]{1,0:T(8,128)(2,1)S(1)}, u32[]{:S(2)}, u32[]{:S(2)}) collective-permute-start(bf16[128,2048]{1,0:T(8,128)(2,1)} %shard_map.47), channel_id=1, source_target_pairs={{0,3},{1,0},{2,1},{3,2},{4,7},{5,4},{6,5},{7,6},{8,11},{9,8},{10,9... | collective-permute-start | bytes 1572872 | tf_op jit(solution)/shard_map/ppermute | solution.py:152
  93.4 0.7 pad_add_fusion.3.meta_ref
  94.0 0.6 pad_add_fusion.2.meta_ref
  94.6 0.8 copy-done.4
  95.4 9.1 %shard_map.48 = bf16[128,2048]{1,0:T(8,128)(2,1)} custom-call(s32[3]{0:T(128)} %pad_add_fusion.2.meta_ref, s32[4096]{0:T(1024)} %doc_ref.7, bf16[128,2048]{1,0:T(8,128)(2,1)} %copy-done.4, bf16[8,512,256]{2,1,0:T(8,128)(2,1)} %bitcast.33, bf16[8,256,512]{2,1,0:T(8,128)(2,1)} %bitcast.37, s32[1,128]{1,0:T(1,128)} %bitcast.56), custom_call_target="tpu_custom_call" | custom-call | tf_op jit(solution)/shard_map/pallas_call | solution.py:94
  104.6 0.0 collective-permute-start.6
  104.6 0.6 pad_add_fusion.meta_ref
  105.1 0.0 collective-permute-done.7.q_ref
  105.1 0.8 copy-done.3
  105.9 9.1 %shard_map.49 = bf16[128,2048]{1,0:T(8,128)(2,1)} custom-call(s32[3]{0:T(128)} %pad_add_fusion.3.meta_ref, s32[4096]{0:T(1024)} %doc_ref.7, bf16[128,2048]{1,0:T(8,128)(2,1)} %copy-done.3, bf16[8,512,256]{2,1,0:T(8,128)(2,1)} %bitcast.34, bf16[8,256,512]{2,1,0:T(8,128)(2,1)} %bitcast.38, s32[1,128]{1,0:T(1,128)} %bitcast.51), custom_call_target="tpu_custom_call" | custom-call | tf_op jit(solution)/shard_map/pallas_call | solution.py:94
  115.1 1.1 collective-permute-start.8
  116.2 9.1 %shard_map.46 = bf16[128,2048]{1,0:T(8,128)(2,1)} custom-call(s32[3]{0:T(128)} %pad_add_fusion.meta_ref, s32[4096]{0:T(1024)} %doc_ref.7, bf16[128,2048]{1,0:T(8,128)(2,1)} %get-tuple-element.11.q_ref, bf16[8,512,256]{2,1,0:T(8,128)(2,1)} %bitcast.35, bf16[8,256,512]{2,1,0:T(8,128)(2,1)} %bitcast.39, s32[1,128]{1,0:T(1,128)} %bitcast.46), custom_call_target="tpu_custom_call" | custom-call | tf_op jit(solution)/shard_map/pallas_call | solution.py:94
  125.3 0.2 broadcast_in_dim.4
  125.5 0.8 copy-done.1
  126.4 0.0 collective-permute-done.4
  126.4 14.5 %collective-permute-done.6 = bf16[128,2048]{1,0:T(8,128)(2,1)S(1)} collective-permute-done((bf16[128,2048]{1,0:T(8,128)(2,1)}, bf16[128,2048]{1,0:T(8,128)(2,1)S(1)}, u32[]{:S(2)}, u32[]{:S(2)}) %collective-permute-start.6) | collective-permute-done | bytes 524320 | tf_op jit(solution)/shard_map/ppermute | solution.py:152
  141.0 0.0 copy-start
  141.0 1.3 copy-done
  142.3 0.8 constant_dynamic-update-slice_fusion
  (26 shorter events, 0.4 us)
Async XLA Ops:
  6.5 44.6 %all-gather.5.cloned.1.call-start = ((), (), s32[]{:S(2)}) async-start(), calls=%async_computation | async-start | bytes 2359296 | tf_op jit(solution)/shard_map/all_gather | solution.py:130
  7.6 8.3 %collective-permute-start = (bf16[128,2,256]{2,0,1:T(8,128)(2,1)S(1)}, bf16[128,2,256]{2,0,1:T(8,128)(2,1)S(1)}, u32[]{:S(2)}, u32[]{:S(2)}) collective-permute-start(bf16[128,2,256]{2,0,1:T(8,128)(2,1)S(1)} %get-tuple-element.17), channel_id=1, source_target_pairs={{0,1},{1,2},{2,3},{3,0},{4,5},{5,6},{6,7},{7,4},{8,9},{9,10},{10,1... | collective-permute-start | bytes 393224 | tf_op jit(solution)/shard_map/ppermute | solution.py:128
  9.3 11.2 %collective-permute-start.1 = (bf16[128,2,256]{2,0,1:T(8,128)(2,1)S(1)}, bf16[128,2,256]{2,0,1:T(8,128)(2,1)S(1)}, u32[]{:S(2)}, u32[]{:S(2)}) collective-permute-start(bf16[128,2,256]{2,0,1:T(8,128)(2,1)S(1)} %get-tuple-element.18), channel_id=1, source_target_pairs={{0,2},{1,3},{2,0},{3,1},{4,6},{5,7},{6,4},{7,5},{8,10},{9,11},{10,... | collective-permute-start | bytes 393224 | tf_op jit(solution)/shard_map/ppermute | solution.py:128
  11.9 8.8 %collective-permute-start.2 = (bf16[128,2,256]{2,0,1:T(8,128)(2,1)S(1)}, bf16[128,2,256]{2,0,1:T(8,128)(2,1)S(1)}, u32[]{:S(2)}, u32[]{:S(2)}) collective-permute-start(bf16[128,2,256]{2,0,1:T(8,128)(2,1)S(1)} %get-tuple-element.15), channel_id=1, source_target_pairs={{0,3},{1,0},{2,1},{3,2},{4,7},{5,4},{6,5},{7,6},{8,11},{9,8},{10,9... | collective-permute-start | bytes 393224 | tf_op jit(solution)/shard_map/ppermute | solution.py:128
  13.3 9.2 %copy-start.2 = (bf16[128,8192]{1,0:T(8,128)(2,1)S(1)}, bf16[128,8192]{1,0:T(8,128)(2,1)}, u32[]{:S(2)}) copy-start(bf16[128,8192]{1,0:T(8,128)(2,1)} %param.4) | copy-start | bytes 6291460
  21.7 59.2 %all-gather.7.cloned.1.call-start = ((), (), s32[]{:S(2)}) async-start(), calls=%async_computation.1 | async-start | bytes 2359296 | tf_op jit(solution)/shard_map/all_gather | solution.py:131
  22.5 6.1 %copy-start.6 = (s32[4096]{0:T(1024)S(1)}, s32[4096]{0:T(1024)}, u32[]{:S(2)}) copy-start(s32[4096]{0:T(1024)} %doc_ref.7) | copy-start | bytes 49156
  23.7 31.5 %collective-permute-start.3 = (bf16[128,2048]{1,0:T(8,128)(2,1)}, bf16[128,2048]{1,0:T(8,128)(2,1)S(1)}, u32[]{:S(2)}, u32[]{:S(2)}) collective-permute-start(bf16[128,2048]{1,0:T(8,128)(2,1)} %get-tuple-element.10), channel_id=1, source_target_pairs={{0,1},{1,2},{2,3},{3,0},{4,5},{5,6},{6,7},{7,4},{8,9},{9,10},{10,1... | collective-permute-start | bytes 1572872 | tf_op jit(solution)/shard_map/ppermute | solution.py:148
  26.8 78.3 %collective-permute-start.7 = (bf16[128,2048]{1,0:T(8,128)(2,1)S(1)}, bf16[128,2048]{1,0:T(8,128)(2,1)S(1)}, u32[]{:S(2)}, u32[]{:S(2)}) collective-permute-start(bf16[128,2048]{1,0:T(8,128)(2,1)S(1)} %get-tuple-element.9), channel_id=1, source_target_pairs={{0,3},{1,0},{2,1},{3,2},{4,7},{5,4},{6,5},{7,6},{8,11},{9,8},{10,9... | collective-permute-start | bytes 1572872 | tf_op jit(solution)/shard_map/ppermute | solution.py:148
  28.0 66.6 %collective-permute-start.5 = (bf16[128,2048]{1,0:T(8,128)(2,1)S(1)}, bf16[128,2048]{1,0:T(8,128)(2,1)S(1)}, u32[]{:S(2)}, u32[]{:S(2)}) collective-permute-start(bf16[128,2048]{1,0:T(8,128)(2,1)S(1)} %get-tuple-element.12), channel_id=1, source_target_pairs={{0,2},{1,3},{2,0},{3,1},{4,6},{5,7},{6,4},{7,5},{8,10},{9,11},{10,... | collective-permute-start | bytes 1572872 | tf_op jit(solution)/shard_map/ppermute | solution.py:148
  29.7 25.5 %copy-start.7 = (s32[128]{0:T(128)}, s32[128]{0:T(128)S(1)}, u32[]{:S(2)}) copy-start(s32[128]{0:T(128)S(1)} %get-tuple-element.8) | copy-start | bytes 1540
  29.7 25.5 %copy-start.8 = (s32[128]{0:T(128)}, s32[128]{0:T(128)S(1)}, u32[]{:S(2)}) copy-start(s32[128]{0:T(128)S(1)} %get-tuple-element.5) | copy-start | bytes 1540
  29.7 25.5 %copy-start.9 = (s32[128]{0:T(128)}, s32[128]{0:T(128)S(1)}, u32[]{:S(2)}) copy-start(s32[128]{0:T(128)S(1)} %get-tuple-element.7) | copy-start | bytes 1540
  29.7 25.5 %copy-start.10 = (s32[128]{0:T(128)}, s32[128]{0:T(128)S(1)}, u32[]{:S(2)}) copy-start(s32[128]{0:T(128)S(1)} %get-tuple-element.6) | copy-start | bytes 1540
  55.2 25.7 %copy-start.5 = (bf16[128,2048]{1,0:T(8,128)(2,1)}, bf16[128,2048]{1,0:T(8,128)(2,1)S(1)}, u32[]{:S(2)}) copy-start(bf16[128,2048]{1,0:T(8,128)(2,1)S(1)} %collective-permute-done.3.q_ref) | copy-start | bytes 1572868
  90.0 36.3 %collective-permute-start.4 = (bf16[128,2048]{1,0:T(8,128)(2,1)}, bf16[128,2048]{1,0:T(8,128)(2,1)S(1)}, u32[]{:S(2)}, u32[]{:S(2)}) collective-permute-start(bf16[128,2048]{1,0:T(8,128)(2,1)} %shard_map.47), channel_id=1, source_target_pairs={{0,3},{1,0},{2,1},{3,2},{4,7},{5,4},{6,5},{7,6},{8,11},{9,8},{10,9... | collective-permute-start | bytes 1572872 | tf_op jit(solution)/shard_map/ppermute | solution.py:152
  94.6 0.8 copy-start.4
  104.6 36.4 %collective-permute-start.6 = (bf16[128,2048]{1,0:T(8,128)(2,1)}, bf16[128,2048]{1,0:T(8,128)(2,1)S(1)}, u32[]{:S(2)}, u32[]{:S(2)}) collective-permute-start(bf16[128,2048]{1,0:T(8,128)(2,1)} %shard_map.48), channel_id=1, source_target_pairs={{0,2},{1,3},{2,0},{3,1},{4,6},{5,7},{6,4},{7,5},{8,10},{9,11},{10,... | collective-permute-start | bytes 1572872 | tf_op jit(solution)/shard_map/ppermute | solution.py:152
  105.1 0.8 copy-start.3
  115.1 26.0 %collective-permute-start.8 = (bf16[128,2048]{1,0:T(8,128)(2,1)}, bf16[128,2048]{1,0:T(8,128)(2,1)S(1)}, u32[]{:S(2)}, u32[]{:S(2)}) collective-permute-start(bf16[128,2048]{1,0:T(8,128)(2,1)} %shard_map.49), channel_id=1, source_target_pairs={{0,1},{1,2},{2,3},{3,0},{4,5},{5,6},{6,7},{7,4},{8,9},{9,10},{10,1... | collective-permute-start | bytes 1572872 | tf_op jit(solution)/shard_map/ppermute | solution.py:152
  125.3 1.0 copy-start.1
  141.0 1.3 copy-start
Sparse Core Ops, SparseCore 0:
  21.8 29.2 all-gather.4
  53.0 27.8 all-gather.6

commit v4 on v1

--- a/solution.py
+++ b/solution.py
@@ -127,7 +127,9 @@
         if t:
             piece = lax.ppermute(piece, "head", [(i, (i + t) % head_count) for i in range(head_count)])
         local = lax.dynamic_update_slice_in_dim(local, piece, ((head - t) % head_count) * sub, axis=0)
-    whole = lax.all_gather(local, "seq", axis=0, tiled=True)
+    seq_count = lax.axis_size("seq")
+    copies = jnp.broadcast_to(local[None], (seq_count,) + local.shape).reshape((-1,) + local.shape[1:])
+    whole = lax.all_to_all(copies, "seq", split_axis=0, concat_axis=0, tiled=True)
     return whole[:, 0, :], whole[:, 1, :].T
 
 

time: 147 us -> 164 us (1.12)
  the two profiles are of different devices: /device:TPU:5 before, /device:TPU:6 now
where the time goes in v4:
time: 164 us; the launch traced here: 165 us
  waiting for transfers between devices  53.6 us (33%)
  Pallas kernels  49.7 us (30%)
  local copies, waits for them, and re-layouts  35.4 us (22%)
  starting transfers between devices  20.4 us (12%)
  other arithmetic  4.69 us (3%)
    pallas_call x4, Pallas kernels, attend(): pl.pallas_call(kernel, out_shape=jax.ShapeDtypeStruct((q_rows, width), jn...  49.7 us
    all_to_all x1, waiting for transfers between devices, gather_kv(): lax.all_to_all(copies, 'seq', split_axis=0, concat_axis=0, tiled=True)  38.2 us
    unnamed x24, local copies, waits for them, and re-layouts  18.2 us
    slice x1, local copies, waits for them, and re-layouts, gather_kv(): return (whole[:, 0, :], whole[:, 1, :].T)  9.83 us
    ppermute x3, waiting for transfers between devices, body(): lax.ppermute(out_tile, 'head', [(i, (i - t) % head_count) for i in range(...  8.08 us
    ppermute x3, waiting for transfers between devices, gather_kv(): lax.ppermute(piece, 'head', [(i, (i + t) % head_count) for i in range(hea...  7.28 us
    ppermute x3, starting transfers between devices, gather_kv(): lax.ppermute(piece, 'head', [(i, (i + t) % head_count) for i in range(hea...  5.57 us
    all_to_all x1, starting transfers between devices, gather_kv(): lax.all_to_all(copies, 'seq', split_axis=0, concat_axis=0, tiled=True)  5.06 us
  transfers between devices with their start and end apart: 10, of which 4 were waited for; matrix products, arithmetic and copies ran while one was open for 18% of the time, Pallas kernels for 30%

profile of v4, /device:TPU:6, one launch (start us, length us, event | category | flops | bytes accessed | tf_op | source)
XLA Modules:
  0.0 164.7 jit_solution(9303324672205543964)
XLA Ops:
  0.0 1.1 fusion
  1.2 1.6 collective-permute-start
  2.8 2.6 %collective-permute-start.1 = (bf16[128,2,256]{2,0,1:T(8,128)(2,1)S(1)}, bf16[128,2,256]{2,0,1:T(8,128)(2,1)S(1)}, u32[]{:S(2)}, u32[]{:S(2)}) collective-permute-start(bf16[128,2,256]{2,0,1:T(8,128)(2,1)S(1)} %get-tuple-element.18), channel_id=1, source_target_pairs={{0,2},{1,3},{2,0},{3,1},{4,6},{5,7},{6,4},{7,5},{8,10},{9,11},{10,... | collective-permute-start | bytes 393224 | tf_op jit(solution)/shard_map/ppermute | solution.py:128
  5.4 1.3 collective-permute-start.2
  6.7 2.8 %collective-permute-done = bf16[128,2,256]{2,0,1:T(8,128)(2,1)S(1)} collective-permute-done((bf16[128,2,256]{2,0,1:T(8,128)(2,1)S(1)}, bf16[128,2,256]{2,0,1:T(8,128)(2,1)S(1)}, u32[]{:S(2)}, u32[]{:S(2)}) %collective-permute-start) | collective-permute-done | bytes 131104 | tf_op jit(solution)/shard_map/ppermute | solution.py:128
  9.5 4.5 %collective-permute-done.1 = bf16[128,2,256]{2,0,1:T(8,128)(2,1)S(1)} collective-permute-done((bf16[128,2,256]{2,0,1:T(8,128)(2,1)S(1)}, bf16[128,2,256]{2,0,1:T(8,128)(2,1)S(1)}, u32[]{:S(2)}, u32[]{:S(2)}) %collective-permute-start.1) | collective-permute-done | bytes 131104 | tf_op jit(solution)/shard_map/ppermute | solution.py:128
  14.0 0.5 copy.15
  14.6 0.0 collective-permute-done.2
  14.6 0.2 copy_dynamic-update-slice_fusion
  14.8 4.1 %broadcast_in_dim.8 = bf16[8,512,2,256]{3,2,1,0:T(2,128)(2,1)} broadcast(bf16[512,2,256]{2,1,0:T(2,128)(2,1)S(1)} %copy_dynamic-update-slice_fusion), dimensions={1,2,3} | broadcast | bytes 4718592 | tf_op jit(solution)/shard_map/broadcast_in_dim | solution.py:131
  18.9 5.1 %all-to-all-start = ((bf16[4096,2,256]{2,1,0:T(2,128)(2,1)}), bf16[4096,2,256]{2,1,0:T(2,128)(2,1)}, u32[]{:S(2)}, u32[]{:S(2)}) async-start(bf16[4096,2,256]{2,1,0:T(2,128)(2,1)} %bitcast.41), calls=%async_computation | async-start | bytes 8388608 | tf_op jit(solution)/shard_map/all_to_all | solution.py:132
  24.0 1.2 constant_dynamic-slice_fusion
  25.2 4.3 %collective-permute-start.7 = (bf16[128,2048]{1,0:T(8,128)(2,1)S(1)}, bf16[128,2048]{1,0:T(8,128)(2,1)S(1)}, u32[]{:S(2)}, u32[]{:S(2)}) collective-permute-start(bf16[128,2048]{1,0:T(8,128)(2,1)S(1)} %get-tuple-element.11), channel_id=1, source_target_pairs={{0,3},{1,0},{2,1},{3,2},{4,7},{5,4},{6,5},{7,6},{8,11},{9,8},{10,9... | collective-permute-start | bytes 1572872 | tf_op jit(solution)/shard_map/ppermute | solution.py:149
  29.5 0.0 collective-permute-start.5
  29.5 0.6 collective-permute-start.3
  30.1 0.1 fusion.6
  30.2 1.0 convert_reduce_fusion
  31.2 0.0 copy-start.8
  31.2 0.0 copy-start.9
  31.9 0.7 pad_add_fusion.1.meta_ref
  32.6 38.2 %all-to-all-done = bf16[4096,2,256]{2,1,0:T(2,128)(2,1)} async-done(((bf16[4096,2,256]{2,1,0:T(2,128)(2,1)}), bf16[4096,2,256]{2,1,0:T(2,128)(2,1)}, u32[]{:S(2)}, u32[]{:S(2)}) %all-to-all-start) | async-done | bytes 4194336 | tf_op jit(solution)/shard_map/all_to_all | solution.py:132
  70.8 9.8 %fusion.5 = (bf16[4096,1,256]{2,1,0:T(2,128)(2,1)}, bf16[4096,1,256]{2,1,0:T(2,128)(2,1)}) fusion(bf16[4096,2,256]{2,1,0:T(2,128)(2,1)} %all-to-all-done), kind=kLoop, calls=%fused_computation.33 | loop fusion | bytes 8388608 | tf_op jit(solution)/shard_map/slice | solution.py:133
  80.7 9.8 %copy.20 = bf16[4096,1,256]{0,2,1:T(8,128)(2,1)} copy(bf16[4096,1,256]{2,1,0:T(2,128)(2,1)} %get-tuple-element.9) | data formatting | bytes 4194304
  90.5 3.9 %copy.23 = bf16[4096,1,256]{2,0,1:T(8,128)(2,1)} copy(bf16[4096,1,256]{2,1,0:T(2,128)(2,1)} %get-tuple-element.10) | data formatting | bytes 4194304
  94.3 0.0 collective-permute-done.3.q_ref
  94.3 0.8 copy-done.5
  95.2 12.4 %shard_map.47 = bf16[128,2048]{1,0:T(8,128)(2,1)} custom-call(s32[3]{0:T(128)} %pad_add_fusion.1.meta_ref, s32[4096]{0:T(1024)} %doc_ref.7, bf16[128,2048]{1,0:T(8,128)(2,1)} %copy-done.5, bf16[4096,256]{1,0:T(8,128)(2,1)} %bitcast.37, bf16[256,4096]{1,0:T(8,128)(2,1)} %bitcast.33, s32[1,128]{1,0:T(1,128)} %bitcast.63), custom_call_target="tpu_custom_call" | custom-call | tf_op jit(solution)/shard_map/pallas_call | solution.py:94
  107.6 4.3 %collective-permute-start.4 = (bf16[128,2048]{1,0:T(8,128)(2,1)}, bf16[128,2048]{1,0:T(8,128)(2,1)S(1)}, u32[]{:S(2)}, u32[]{:S(2)}) collective-permute-start(bf16[128,2048]{1,0:T(8,128)(2,1)} %shard_map.47), channel_id=1, source_target_pairs={{0,3},{1,0},{2,1},{3,2},{4,7},{5,4},{6,5},{7,6},{8,11},{9,8},{10,9... | collective-permute-start | bytes 1572872 | tf_op jit(solution)/shard_map/ppermute | solution.py:153
  111.9 0.6 pad_add_fusion.3.meta_ref
  112.5 0.7 pad_add_fusion.2.meta_ref
  113.2 0.0 collective-permute-done.5.q_ref
  113.2 0.8 copy-done.4
  114.0 12.4 %shard_map.48 = bf16[128,2048]{1,0:T(8,128)(2,1)} custom-call(s32[3]{0:T(128)} %pad_add_fusion.2.meta_ref, s32[4096]{0:T(1024)} %doc_ref.7, bf16[128,2048]{1,0:T(8,128)(2,1)} %copy-done.4, bf16[4096,256]{1,0:T(8,128)(2,1)} %bitcast.38, bf16[256,4096]{1,0:T(8,128)(2,1)} %bitcast.34, s32[1,128]{1,0:T(1,128)} %bitcast.58), custom_call_target="tpu_custom_call" | custom-call | tf_op jit(solution)/shard_map/pallas_call | solution.py:94
  126.4 0.0 collective-permute-start.6
  126.4 0.7 pad_add_fusion.meta_ref
  127.1 0.0 collective-permute-done.7.q_ref
  127.1 0.8 copy-done.3
  127.9 12.4 %shard_map.49 = bf16[128,2048]{1,0:T(8,128)(2,1)} custom-call(s32[3]{0:T(128)} %pad_add_fusion.3.meta_ref, s32[4096]{0:T(1024)} %doc_ref.7, bf16[128,2048]{1,0:T(8,128)(2,1)} %copy-done.3, bf16[4096,256]{1,0:T(8,128)(2,1)} %bitcast.39, bf16[256,4096]{1,0:T(8,128)(2,1)} %bitcast.35, s32[1,128]{1,0:T(1,128)} %bitcast.53), custom_call_target="tpu_custom_call" | custom-call | tf_op jit(solution)/shard_map/pallas_call | solution.py:94
  140.3 0.6 collective-permute-start.8
  140.8 12.4 %shard_map.46 = bf16[128,2048]{1,0:T(8,128)(2,1)} custom-call(s32[3]{0:T(128)} %pad_add_fusion.meta_ref, s32[4096]{0:T(1024)} %doc_ref.7, bf16[128,2048]{1,0:T(8,128)(2,1)} %get-tuple-element.13.q_ref, bf16[4096,256]{1,0:T(8,128)(2,1)} %bitcast.40, bf16[256,4096]{1,0:T(8,128)(2,1)} %bitcast.36, s32[1,128]{1,0:T(1,128)} %bitcast.48), custom_call_target="tpu_custom_call" | custom-call | tf_op jit(solution)/shard_map/pallas_call | solution.py:94
  153.2 0.2 broadcast_in_dim.6
  153.4 0.8 copy-done.1
  154.3 0.0 collective-permute-done.4
  154.4 8.1 %collective-permute-done.6 = bf16[128,2048]{1,0:T(8,128)(2,1)S(1)} collective-permute-done((bf16[128,2048]{1,0:T(8,128)(2,1)}, bf16[128,2048]{1,0:T(8,128)(2,1)S(1)}, u32[]{:S(2)}, u32[]{:S(2)}) %collective-permute-start.6) | collective-permute-done | bytes 524320 | tf_op jit(solution)/shard_map/ppermute | solution.py:153
  162.5 0.0 copy-start
  162.5 0.0 collective-permute-done.8
  162.6 1.3 copy-done
  163.9 0.8 constant_dynamic-update-slice_fusion
  (20 shorter events, 0.2 us)
Async XLA Ops:
  1.2 8.3 %collective-permute-start = (bf16[128,2,256]{2,0,1:T(8,128)(2,1)S(1)}, bf16[128,2,256]{2,0,1:T(8,128)(2,1)S(1)}, u32[]{:S(2)}, u32[]{:S(2)}) collective-permute-start(bf16[128,2,256]{2,0,1:T(8,128)(2,1)S(1)} %get-tuple-element.17), channel_id=1, source_target_pairs={{0,1},{1,2},{2,3},{3,0},{4,5},{5,6},{6,7},{7,4},{8,9},{9,10},{10,1... | collective-permute-start | bytes 393224 | tf_op jit(solution)/shard_map/ppermute | solution.py:128
  2.8 11.2 %collective-permute-start.1 = (bf16[128,2,256]{2,0,1:T(8,128)(2,1)S(1)}, bf16[128,2,256]{2,0,1:T(8,128)(2,1)S(1)}, u32[]{:S(2)}, u32[]{:S(2)}) collective-permute-start(bf16[128,2,256]{2,0,1:T(8,128)(2,1)S(1)} %get-tuple-element.18), channel_id=1, source_target_pairs={{0,2},{1,3},{2,0},{3,1},{4,6},{5,7},{6,4},{7,5},{8,10},{9,11},{10,... | collective-permute-start | bytes 393224 | tf_op jit(solution)/shard_map/ppermute | solution.py:128
  5.4 9.2 %collective-permute-start.2 = (bf16[128,2,256]{2,0,1:T(8,128)(2,1)S(1)}, bf16[128,2,256]{2,0,1:T(8,128)(2,1)S(1)}, u32[]{:S(2)}, u32[]{:S(2)}) collective-permute-start(bf16[128,2,256]{2,0,1:T(8,128)(2,1)S(1)} %get-tuple-element.15), channel_id=1, source_target_pairs={{0,3},{1,0},{2,1},{3,2},{4,7},{5,4},{6,5},{7,6},{8,11},{9,8},{10,9... | collective-permute-start | bytes 393224 | tf_op jit(solution)/shard_map/ppermute | solution.py:128
  18.9 5.1 %copy-start.2 = (bf16[128,8192]{1,0:T(8,128)(2,1)S(1)}, bf16[128,8192]{1,0:T(8,128)(2,1)}, u32[]{:S(2)}) copy-start(bf16[128,8192]{1,0:T(8,128)(2,1)} %param.4) | copy-start | bytes 6291460
  18.9 52.0 %all-to-all-start = ((bf16[4096,2,256]{2,1,0:T(2,128)(2,1)}), bf16[4096,2,256]{2,1,0:T(2,128)(2,1)}, u32[]{:S(2)}, u32[]{:S(2)}) async-start(bf16[4096,2,256]{2,1,0:T(2,128)(2,1)} %bitcast.41), calls=%async_computation | async-start | bytes 8388608 | tf_op jit(solution)/shard_map/all_to_all | solution.py:132
  24.0 6.1 %copy-start.6 = (s32[4096]{0:T(1024)S(1)}, s32[4096]{0:T(1024)}, u32[]{:S(2)}) copy-start(s32[4096]{0:T(1024)} %doc_ref.7) | copy-start | bytes 49156
  25.2 101.9 %collective-permute-start.7 = (bf16[128,2048]{1,0:T(8,128)(2,1)S(1)}, bf16[128,2048]{1,0:T(8,128)(2,1)S(1)}, u32[]{:S(2)}, u32[]{:S(2)}) collective-permute-start(bf16[128,2048]{1,0:T(8,128)(2,1)S(1)} %get-tuple-element.11), channel_id=1, source_target_pairs={{0,3},{1,0},{2,1},{3,2},{4,7},{5,4},{6,5},{7,6},{8,11},{9,8},{10,9... | collective-permute-start | bytes 1572872 | tf_op jit(solution)/shard_map/ppermute | solution.py:149
  29.5 83.7 %collective-permute-start.5 = (bf16[128,2048]{1,0:T(8,128)(2,1)}, bf16[128,2048]{1,0:T(8,128)(2,1)S(1)}, u32[]{:S(2)}, u32[]{:S(2)}) collective-permute-start(bf16[128,2048]{1,0:T(8,128)(2,1)} %get-tuple-element.14), channel_id=1, source_target_pairs={{0,2},{1,3},{2,0},{3,1},{4,6},{5,7},{6,4},{7,5},{8,10},{9,11},{10,... | collective-permute-start | bytes 1572872 | tf_op jit(solution)/shard_map/ppermute | solution.py:149
  29.5 64.8 %collective-permute-start.3 = (bf16[128,2048]{1,0:T(8,128)(2,1)}, bf16[128,2048]{1,0:T(8,128)(2,1)S(1)}, u32[]{:S(2)}, u32[]{:S(2)}) collective-permute-start(bf16[128,2048]{1,0:T(8,128)(2,1)} %get-tuple-element.12), channel_id=1, source_target_pairs={{0,1},{1,2},{2,3},{3,0},{4,5},{5,6},{6,7},{7,4},{8,9},{9,10},{10,1... | collective-permute-start | bytes 1572872 | tf_op jit(solution)/shard_map/ppermute | solution.py:149
  31.2 49.5 %copy-start.7 = (s32[128]{0:T(128)}, s32[128]{0:T(128)S(1)}, u32[]{:S(2)}) copy-start(s32[128]{0:T(128)S(1)} %get-tuple-element.8) | copy-start | bytes 1540
  31.2 49.5 %copy-start.8 = (s32[128]{0:T(128)}, s32[128]{0:T(128)S(1)}, u32[]{:S(2)}) copy-start(s32[128]{0:T(128)S(1)} %get-tuple-element.5) | copy-start | bytes 1540
  31.2 49.5 %copy-start.9 = (s32[128]{0:T(128)}, s32[128]{0:T(128)S(1)}, u32[]{:S(2)}) copy-start(s32[128]{0:T(128)S(1)} %get-tuple-element.7) | copy-start | bytes 1540
  31.2 49.5 %copy-start.10 = (s32[128]{0:T(128)}, s32[128]{0:T(128)S(1)}, u32[]{:S(2)}) copy-start(s32[128]{0:T(128)S(1)} %get-tuple-element.6) | copy-start | bytes 1540
  94.3 0.8 copy-start.5
  107.6 46.8 %collective-permute-start.4 = (bf16[128,2048]{1,0:T(8,128)(2,1)}, bf16[128,2048]{1,0:T(8,128)(2,1)S(1)}, u32[]{:S(2)}, u32[]{:S(2)}) collective-permute-start(bf16[128,2048]{1,0:T(8,128)(2,1)} %shard_map.47), channel_id=1, source_target_pairs={{0,3},{1,0},{2,1},{3,2},{4,7},{5,4},{6,5},{7,6},{8,11},{9,8},{10,9... | collective-permute-start | bytes 1572872 | tf_op jit(solution)/shard_map/ppermute | solution.py:153
  113.2 0.8 copy-start.4
  126.4 36.1 %collective-permute-start.6 = (bf16[128,2048]{1,0:T(8,128)(2,1)}, bf16[128,2048]{1,0:T(8,128)(2,1)S(1)}, u32[]{:S(2)}, u32[]{:S(2)}) collective-permute-start(bf16[128,2048]{1,0:T(8,128)(2,1)} %shard_map.48), channel_id=1, source_target_pairs={{0,2},{1,3},{2,0},{3,1},{4,6},{5,7},{6,4},{7,5},{8,10},{9,11},{10,... | collective-permute-start | bytes 1572872 | tf_op jit(solution)/shard_map/ppermute | solution.py:153
  127.1 0.8 copy-start.3
  140.3 22.3 %collective-permute-start.8 = (bf16[128,2048]{1,0:T(8,128)(2,1)}, bf16[128,2048]{1,0:T(8,128)(2,1)S(1)}, u32[]{:S(2)}, u32[]{:S(2)}) collective-permute-start(bf16[128,2048]{1,0:T(8,128)(2,1)} %shard_map.49), channel_id=1, source_target_pairs={{0,1},{1,2},{2,3},{3,0},{4,5},{5,6},{6,7},{7,4},{8,9},{9,10},{10,1... | collective-permute-start | bytes 1572872 | tf_op jit(solution)/shard_map/ppermute | solution.py:153
  153.2 1.0 copy-start.1
  162.5 1.3 copy-start

commit v5 on v1

--- a/solution.py
+++ b/solution.py
@@ -115,6 +115,23 @@
     )(meta, doc_ids, q_tile, keys, values_t, query_start)
 
 
+def gather_seq(local):
+    seq_count = lax.axis_size("seq")
+    assert seq_count & (seq_count - 1) == 0
+    seq = lax.axis_index("seq")
+    rows = local.shape[0]
+    whole = jnp.zeros((seq_count * rows,) + local.shape[1:], local.dtype)
+    whole = lax.dynamic_update_slice_in_dim(whole, local, seq * rows, axis=0)
+    span = 1
+    while span < seq_count:
+        base = (seq // span) * span
+        held = lax.dynamic_slice_in_dim(whole, base * rows, span * rows, axis=0)
+        got = lax.ppermute(held, "seq", [(i, i ^ span) for i in range(seq_count)])
+        whole = lax.dynamic_update_slice_in_dim(whole, got, (base ^ span) * rows, axis=0)
+        span *= 2
+    return whole
+
+
 def gather_kv(key_rows, value_rows):
     head_count = lax.axis_size("head")
     head = lax.axis_index("head")
@@ -127,7 +144,7 @@
         if t:
             piece = lax.ppermute(piece, "head", [(i, (i + t) % head_count) for i in range(head_count)])
         local = lax.dynamic_update_slice_in_dim(local, piece, ((head - t) % head_count) * sub, axis=0)
-    whole = lax.all_gather(local, "seq", axis=0, tiled=True)
+    whole = gather_seq(local)
     return whole[:, 0, :], whole[:, 1, :].T
 
 

time: 147 us -> 179 us (1.22)
  the two profiles are of different devices: /device:TPU:5 before, /device:TPU:6 now
where the time goes in v5:
time: 179 us; the launch traced here: 177 us
  waiting for transfers between devices  78.7 us (44%)
  Pallas kernels  49.7 us (28%)
  local copies, waits for them, and re-layouts  27.1 us (15%)
  starting transfers between devices  16.6 us (9%)
  other arithmetic  3.58 us (2%)
    ppermute x3, waiting for transfers between devices, gather_seq(): got = lax.ppermute(held, 'seq', [(i, i ^ span) for i in range(seq_count)])  62.8 us
    pallas_call x4, Pallas kernels, attend(): pl.pallas_call(kernel, out_shape=jax.ShapeDtypeStruct((q_rows, width), jn...  49.7 us
    ppermute x3, waiting for transfers between devices, body(): lax.ppermute(out_tile, 'head', [(i, (i - t) % head_count) for i in range(...  8.65 us
    unnamed x22, local copies, waits for them, and re-layouts  7.95 us
    ppermute x3, waiting for transfers between devices, gather_kv(): lax.ppermute(piece, 'head', [(i, (i + t) % head_count) for i in range(hea...  7.26 us
    ppermute x3, starting transfers between devices, gather_kv(): lax.ppermute(piece, 'head', [(i, (i + t) % head_count) for i in range(hea...  5.57 us
    ppermute x3, starting transfers between devices, body(): lax.ppermute(out_tile, 'head', [(i, (i - t) % head_count) for i in range(...  4.91 us
    ppermute x3, starting transfers between devices, body(): lax.ppermute(piece, 'head', [(i, (i + t) % head_count) for i in range(hea...  4.91 us
  transfers between devices with their start and end apart: 12, of which 6 were waited for; matrix products, arithmetic and copies ran while one was open for 8% of the time, Pallas kernels for 28%

profile of v5, /device:TPU:6, one launch (start us, length us, event | category | flops | bytes accessed | tf_op | source)
XLA Modules:
  0.0 176.7 jit_solution(5357334907459939682)
XLA Ops:
  0.0 1.1 copy.11
  1.1 1.1 copy.12
  2.3 0.1 fusion
  2.4 1.6 collective-permute-start
  4.0 2.6 %collective-permute-start.1 = (bf16[128,2,256]{0,2,1:T(8,128)(2,1)S(1)}, bf16[128,2,256]{0,2,1:T(8,128)(2,1)S(1)}, u32[]{:S(2)}, u32[]{:S(2)}) collective-permute-start(bf16[128,2,256]{0,2,1:T(8,128)(2,1)S(1)} %get-tuple-element.18), channel_id=1, source_target_pairs={{0,2},{1,3},{2,0},{3,1},{4,6},{5,7},{6,4},{7,5},{8,10},{9,11},{10,... | collective-permute-start | bytes 393224 | tf_op jit(solution)/shard_map/ppermute | solution.py:145
  6.6 1.3 collective-permute-start.2
  8.0 2.8 %collective-permute-done = bf16[128,2,256]{0,2,1:T(8,128)(2,1)S(1)} collective-permute-done((bf16[128,2,256]{0,2,1:T(8,128)(2,1)S(1)}, bf16[128,2,256]{0,2,1:T(8,128)(2,1)S(1)}, u32[]{:S(2)}, u32[]{:S(2)}) %collective-permute-start) | collective-permute-done | bytes 131104 | tf_op jit(solution)/shard_map/ppermute | solution.py:145
  10.8 4.5 %collective-permute-done.1 = bf16[128,2,256]{0,2,1:T(8,128)(2,1)S(1)} collective-permute-done((bf16[128,2,256]{0,2,1:T(8,128)(2,1)S(1)}, bf16[128,2,256]{0,2,1:T(8,128)(2,1)S(1)}, u32[]{:S(2)}, u32[]{:S(2)}) %collective-permute-start.1) | collective-permute-done | bytes 131104 | tf_op jit(solution)/shard_map/ppermute | solution.py:145
  15.4 0.5 broadcast_in_dim.7
  15.9 0.1 constant_dynamic-update-slice_fusion.7
  15.9 2.0 %copy-done = bf16[4096,2,256]{0,2,1:T(8,128)(2,1)} copy-done((bf16[4096,2,256]{0,2,1:T(8,128)(2,1)}, bf16[4096,2,256]{0,2,1:T(8,128)(2,1)S(1)}, u32[]{:S(2)}) %copy-start) | copy-done | bytes 4194328
  17.9 0.1 collective-permute-start.3
  18.1 1.9 %collective-permute-done.3 = bf16[512,2,256]{0,2,1:T(8,128)(2,1)S(1)} collective-permute-done((bf16[512,2,256]{0,2,1:T(8,128)(2,1)S(1)}, bf16[512,2,256]{0,2,1:T(8,128)(2,1)S(1)}, u32[]{:S(2)}, u32[]{:S(2)}) %collective-permute-start.3) | collective-permute-done | bytes 524320 | tf_op jit(solution)/shard_map/ppermute | solution.py:129
  19.9 0.9 constant_dynamic-update-slice_fusion.6
  20.8 1.3 constant_dynamic-slice_fusion.4
  22.1 0.6 collective-permute-start.4
  22.7 24.7 %collective-permute-done.4 = bf16[1024,2,256]{0,2,1:T(8,128)(2,1)S(1)} collective-permute-done((bf16[1024,2,256]{0,2,1:T(8,128)(2,1)S(1)}, bf16[1024,2,256]{0,2,1:T(8,128)(2,1)S(1)}, u32[]{:S(2)}, u32[]{:S(2)}) %collective-permute-start.4) | collective-permute-done | bytes 1048608 | tf_op jit(solution)/shard_map/ppermute | solution.py:129
  47.4 1.1 constant_dynamic-update-slice_fusion.5
  48.4 3.2 %constant_dynamic-slice_fusion.3 = bf16[2048,2,256]{0,2,1:T(8,128)(2,1)} fusion(bf16[4096,2,256]{0,2,1:T(8,128)(2,1)} %constant_dynamic-update-slice_fusion.5, s32[]{:T(128)S(6)} %select_n.185), kind=kLoop, calls=%fused_computation.27 | loop fusion | bytes 4194308 | tf_op jit(solution)/shard_map/dynamic_slice | solution.py:128
  51.6 0.6 collective-permute-start.5
  52.2 2.9 %constant_dynamic-slice_fusion = (bf16[128,2048]{1,0:T(8,128)(2,1)}, bf16[128,2048]{1,0:T(8,128)(2,1)}, bf16[128,2048]{1,0:T(8,128)(2,1)}, bf16[128,2048]{1,0:T(8,128)(2,1)}) fusion(bf16[128,8192]{1,0:T(8,128)(2,1)} %param.4, s32[]{:T(128)S(6)} %select_n.198, s32[]{:T(128)S(6)} %select_n.190, s32[]{:T(128)S(6)} %select_n.164, s32[]{:T(128)S(6)} %select_n.194), kind=kLoop, calls=%fused_computation.20 | loop fusion | bytes 4194320 | tf_op jit(solution)/shard_map/dynamic_slice | solution.py:162
  55.1 4.3 %collective-permute-start.10 = (bf16[128,2048]{1,0:T(8,128)(2,1)}, bf16[128,2048]{1,0:T(8,128)(2,1)S(1)}, u32[]{:S(2)}, u32[]{:S(2)}) collective-permute-start(bf16[128,2048]{1,0:T(8,128)(2,1)} %get-tuple-element.11), channel_id=1, source_target_pairs={{0,3},{1,0},{2,1},{3,2},{4,7},{5,4},{6,5},{7,6},{8,11},{9,8},{10,9... | collective-permute-start | bytes 1572872 | tf_op jit(solution)/shard_map/ppermute | solution.py:164
  59.4 0.3 collective-permute-start.8
  59.7 0.2 collective-permute-start.6
  60.0 0.1 fusion.5
  60.1 1.0 convert_reduce_fusion
  61.8 0.6 pad_add_fusion.1.meta_ref
  62.4 36.2 %collective-permute-done.5 = bf16[2048,2,256]{0,2,1:T(8,128)(2,1)S(1)} collective-permute-done((bf16[2048,2,256]{0,2,1:T(8,128)(2,1)}, bf16[2048,2,256]{0,2,1:T(8,128)(2,1)S(1)}, u32[]{:S(2)}, u32[]{:S(2)}) %collective-permute-start.5) | collective-permute-done | bytes 2097184 | tf_op jit(solution)/shard_map/ppermute | solution.py:129
  98.6 1.5 constant_dynamic-update-slice_fusion.4
  100.2 3.9 %slice_bitcast_fusion = (bf16[256,4096]{1,0:T(8,128)(2,1)}, bf16[4096,256]{0,1:T(8,128)(2,1)S(1)}) fusion(bf16[4096,2,256]{0,2,1:T(8,128)(2,1)} %constant_dynamic-update-slice_fusion.4), kind=kLoop, calls=%fused_computation | loop fusion | bytes 8388608 | tf_op jit(solution)/shard_map/transpose | solution.py:148
  104.1 2.5 %copy.13.k_ref = bf16[4096,256]{1,0:T(8,128)(2,1)} copy(bf16[4096,256]{0,1:T(8,128)(2,1)S(1)} %get-tuple-element.10) | data formatting | bytes 4194304 | tf_op jit(solution)/shard_map/squeeze | solution.py:148
  106.6 12.4 %shard_map.47 = bf16[128,2048]{1,0:T(8,128)(2,1)} custom-call(s32[3]{0:T(128)} %pad_add_fusion.1.meta_ref, s32[4096]{0:T(1024)} %doc_ref.7, bf16[128,2048]{1,0:T(8,128)(2,1)} %collective-permute-done.6.q_ref, bf16[4096,256]{1,0:T(8,128)(2,1)} %copy.13.k_ref, bf16[256,4096]{1,0:T(8,128)(2,1)} %get-tuple-element.9.vt_ref, s32[1,128]{1,0:T(1,128)} %bitcast.53), custom_call_target="tpu_custom_call" | custom-call | tf_op jit(solution)/shard_map/pallas_call | solution.py:94
  119.0 4.3 %collective-permute-start.7 = (bf16[128,2048]{1,0:T(8,128)(2,1)}, bf16[128,2048]{1,0:T(8,128)(2,1)S(1)}, u32[]{:S(2)}, u32[]{:S(2)}) collective-permute-start(bf16[128,2048]{1,0:T(8,128)(2,1)} %shard_map.47), channel_id=1, source_target_pairs={{0,3},{1,0},{2,1},{3,2},{4,7},{5,4},{6,5},{7,6},{8,11},{9,8},{10,9... | collective-permute-start | bytes 1572872 | tf_op jit(solution)/shard_map/ppermute | solution.py:168
  123.3 0.6 pad_add_fusion.3.meta_ref
  123.9 0.7 pad_add_fusion.2.meta_ref
  124.6 0.8 copy-done.4
  125.4 12.4 %shard_map.48 = bf16[128,2048]{1,0:T(8,128)(2,1)} custom-call(s32[3]{0:T(128)} %pad_add_fusion.2.meta_ref, s32[4096]{0:T(1024)} %doc_ref.7, bf16[128,2048]{1,0:T(8,128)(2,1)} %copy-done.4, bf16[4096,256]{1,0:T(8,128)(2,1)} %copy.13.k_ref, bf16[256,4096]{1,0:T(8,128)(2,1)} %get-tuple-element.9.vt_ref, s32[1,128]{1,0:T(1,128)} %bitcast.48), custom_call_target="tpu_custom_call" | custom-call | tf_op jit(solution)/shard_map/pallas_call | solution.py:94
  137.8 0.3 collective-permute-start.9
  138.1 0.7 pad_add_fusion.meta_ref
  138.8 0.8 copy-done.3
  139.6 12.4 %shard_map.49 = bf16[128,2048]{1,0:T(8,128)(2,1)} custom-call(s32[3]{0:T(128)} %pad_add_fusion.3.meta_ref, s32[4096]{0:T(1024)} %doc_ref.7, bf16[128,2048]{1,0:T(8,128)(2,1)} %copy-done.3, bf16[4096,256]{1,0:T(8,128)(2,1)} %copy.13.k_ref, bf16[256,4096]{1,0:T(8,128)(2,1)} %get-tuple-element.9.vt_ref, s32[1,128]{1,0:T(1,128)} %bitcast.43), custom_call_target="tpu_custom_call" | custom-call | tf_op jit(solution)/shard_map/pallas_call | solution.py:94
  152.0 0.2 collective-permute-start.11
  152.2 12.4 %shard_map.46 = bf16[128,2048]{1,0:T(8,128)(2,1)} custom-call(s32[3]{0:T(128)} %pad_add_fusion.meta_ref, s32[4096]{0:T(1024)} %doc_ref.7, bf16[128,2048]{1,0:T(8,128)(2,1)} %get-tuple-element.13.q_ref, bf16[4096,256]{1,0:T(8,128)(2,1)} %copy.13.k_ref, bf16[256,4096]{1,0:T(8,128)(2,1)} %get-tuple-element.9.vt_ref, s32[1,128]{1,0:T(1,128)} %bitcast.38), custom_call_target="tpu_custom_call" | custom-call | tf_op jit(solution)/shard_map/pallas_call | solution.py:94
  164.7 0.2 broadcast_in_dim.6
  164.9 0.8 copy-done.2
  165.8 8.6 %collective-permute-done.9 = bf16[128,2048]{1,0:T(8,128)(2,1)S(1)} collective-permute-done((bf16[128,2048]{1,0:T(8,128)(2,1)}, bf16[128,2048]{1,0:T(8,128)(2,1)S(1)}, u32[]{:S(2)}, u32[]{:S(2)}) %collective-permute-start.9) | collective-permute-done | bytes 524320 | tf_op jit(solution)/shard_map/ppermute | solution.py:168
  174.5 1.3 copy-done.1
  175.8 0.8 constant_dynamic-update-slice_fusion
  (29 shorter events, 0.4 us)
Async XLA Ops:
  2.4 8.3 %collective-permute-start = (bf16[128,2,256]{0,2,1:T(8,128)(2,1)S(1)}, bf16[128,2,256]{0,2,1:T(8,128)(2,1)S(1)}, u32[]{:S(2)}, u32[]{:S(2)}) collective-permute-start(bf16[128,2,256]{0,2,1:T(8,128)(2,1)S(1)} %get-tuple-element.17), channel_id=1, source_target_pairs={{0,1},{1,2},{2,3},{3,0},{4,5},{5,6},{6,7},{7,4},{8,9},{9,10},{10,1... | collective-permute-start | bytes 393224 | tf_op jit(solution)/shard_map/ppermute | solution.py:145
  4.0 11.2 %collective-permute-start.1 = (bf16[128,2,256]{0,2,1:T(8,128)(2,1)S(1)}, bf16[128,2,256]{0,2,1:T(8,128)(2,1)S(1)}, u32[]{:S(2)}, u32[]{:S(2)}) collective-permute-start(bf16[128,2,256]{0,2,1:T(8,128)(2,1)S(1)} %get-tuple-element.18), channel_id=1, source_target_pairs={{0,2},{1,3},{2,0},{3,1},{4,6},{5,7},{6,4},{7,5},{8,10},{9,11},{10,... | collective-permute-start | bytes 393224 | tf_op jit(solution)/shard_map/ppermute | solution.py:145
  6.6 8.7 %collective-permute-start.2 = (bf16[128,2,256]{0,2,1:T(8,128)(2,1)S(1)}, bf16[128,2,256]{0,2,1:T(8,128)(2,1)S(1)}, u32[]{:S(2)}, u32[]{:S(2)}) collective-permute-start(bf16[128,2,256]{0,2,1:T(8,128)(2,1)S(1)} %get-tuple-element.15), channel_id=1, source_target_pairs={{0,3},{1,0},{2,1},{3,2},{4,7},{5,4},{6,5},{7,6},{8,11},{9,8},{10,9... | collective-permute-start | bytes 393224 | tf_op jit(solution)/shard_map/ppermute | solution.py:145
  15.9 2.0 %copy-start = (bf16[4096,2,256]{0,2,1:T(8,128)(2,1)}, bf16[4096,2,256]{0,2,1:T(8,128)(2,1)S(1)}, u32[]{:S(2)}) copy-start(bf16[4096,2,256]{0,2,1:T(8,128)(2,1)S(1)} %constant_dynamic-update-slice_fusion.7) | copy-start | bytes 12582916
  17.9 2.0 %collective-permute-start.3 = (bf16[512,2,256]{0,2,1:T(8,128)(2,1)S(1)}, bf16[512,2,256]{0,2,1:T(8,128)(2,1)S(1)}, u32[]{:S(2)}, u32[]{:S(2)}) collective-permute-start(bf16[512,2,256]{0,2,1:T(8,128)(2,1)S(1)} %constant_dynamic-slice_fusion.5), channel_id=1, source_target_pairs={{0,4},{4,0},{8,12},{12,8},{16,20},{20,16},{24,28},{28,24},{1,5},{5... | collective-permute-start | bytes 1572872 | tf_op jit(solution)/shard_map/ppermute | solution.py:129
  22.1 25.3 %collective-permute-start.4 = (bf16[1024,2,256]{0,2,1:T(8,128)(2,1)S(1)}, bf16[1024,2,256]{0,2,1:T(8,128)(2,1)S(1)}, u32[]{:S(2)}, u32[]{:S(2)}) collective-permute-start(bf16[1024,2,256]{0,2,1:T(8,128)(2,1)S(1)} %constant_dynamic-slice_fusion.4), channel_id=1, source_target_pairs={{0,8},{4,12},{8,0},{12,4},{16,24},{20,28},{24,16},{28,20},{1,9},{5... | collective-permute-start | bytes 3145736 | tf_op jit(solution)/shard_map/ppermute | solution.py:129
  51.6 47.1 %collective-permute-start.5 = (bf16[2048,2,256]{0,2,1:T(8,128)(2,1)}, bf16[2048,2,256]{0,2,1:T(8,128)(2,1)S(1)}, u32[]{:S(2)}, u32[]{:S(2)}) collective-permute-start(bf16[2048,2,256]{0,2,1:T(8,128)(2,1)} %constant_dynamic-slice_fusion.3), channel_id=1, source_target_pairs={{0,16},{4,20},{8,24},{12,28},{16,0},{20,4},{24,8},{28,12},{1,17},{... | collective-permute-start | bytes 6291464 | tf_op jit(solution)/shard_map/ppermute | solution.py:129
  52.2 7.8 %copy-start.5 = (s32[4096]{0:T(1024)S(1)}, s32[4096]{0:T(1024)}, u32[]{:S(2)}) copy-start(s32[4096]{0:T(1024)} %doc_ref.7) | copy-start | bytes 49156
  55.1 83.7 %collective-permute-start.10 = (bf16[128,2048]{1,0:T(8,128)(2,1)}, bf16[128,2048]{1,0:T(8,128)(2,1)S(1)}, u32[]{:S(2)}, u32[]{:S(2)}) collective-permute-start(bf16[128,2048]{1,0:T(8,128)(2,1)} %get-tuple-element.11), channel_id=1, source_target_pairs={{0,3},{1,0},{2,1},{3,2},{4,7},{5,4},{6,5},{7,6},{8,11},{9,8},{10,9... | collective-permute-start | bytes 1572872 | tf_op jit(solution)/shard_map/ppermute | solution.py:164
  59.4 65.2 %collective-permute-start.8 = (bf16[128,2048]{1,0:T(8,128)(2,1)}, bf16[128,2048]{1,0:T(8,128)(2,1)S(1)}, u32[]{:S(2)}, u32[]{:S(2)}) collective-permute-start(bf16[128,2048]{1,0:T(8,128)(2,1)} %get-tuple-element.14), channel_id=1, source_target_pairs={{0,2},{1,3},{2,0},{3,1},{4,6},{5,7},{6,4},{7,5},{8,10},{9,11},{10,... | collective-permute-start | bytes 1572872 | tf_op jit(solution)/shard_map/ppermute | solution.py:164
  59.7 46.8 %collective-permute-start.6 = (bf16[128,2048]{1,0:T(8,128)(2,1)}, bf16[128,2048]{1,0:T(8,128)(2,1)}, u32[]{:S(2)}, u32[]{:S(2)}) collective-permute-start(bf16[128,2048]{1,0:T(8,128)(2,1)} %get-tuple-element.12), channel_id=1, source_target_pairs={{0,1},{1,2},{2,3},{3,0},{4,5},{5,6},{6,7},{7,4},{8,9},{9,10},{10,1... | collective-permute-start | bytes 1572872 | tf_op jit(solution)/shard_map/ppermute | solution.py:164
  61.1 39.1 %copy-start.6 = (s32[128]{0:T(128)}, s32[128]{0:T(128)S(1)}, u32[]{:S(2)}) copy-start(s32[128]{0:T(128)S(1)} %get-tuple-element.8) | copy-start | bytes 1540
  61.1 39.1 %copy-start.7 = (s32[128]{0:T(128)}, s32[128]{0:T(128)S(1)}, u32[]{:S(2)}) copy-start(s32[128]{0:T(128)S(1)} %get-tuple-element.5) | copy-start | bytes 1540
  61.1 39.1 %copy-start.8 = (s32[128]{0:T(128)}, s32[128]{0:T(128)S(1)}, u32[]{:S(2)}) copy-start(s32[128]{0:T(128)S(1)} %get-tuple-element.7) | copy-start | bytes 1540
  61.1 39.1 %copy-start.9 = (s32[128]{0:T(128)}, s32[128]{0:T(128)S(1)}, u32[]{:S(2)}) copy-start(s32[128]{0:T(128)S(1)} %get-tuple-element.6) | copy-start | bytes 1540
  119.0 46.8 %collective-permute-start.7 = (bf16[128,2048]{1,0:T(8,128)(2,1)}, bf16[128,2048]{1,0:T(8,128)(2,1)S(1)}, u32[]{:S(2)}, u32[]{:S(2)}) collective-permute-start(bf16[128,2048]{1,0:T(8,128)(2,1)} %shard_map.47), channel_id=1, source_target_pairs={{0,3},{1,0},{2,1},{3,2},{4,7},{5,4},{6,5},{7,6},{8,11},{9,8},{10,9... | collective-permute-start | bytes 1572872 | tf_op jit(solution)/shard_map/ppermute | solution.py:168
  124.6 0.8 copy-start.4
  137.8 36.7 %collective-permute-start.9 = (bf16[128,2048]{1,0:T(8,128)(2,1)}, bf16[128,2048]{1,0:T(8,128)(2,1)S(1)}, u32[]{:S(2)}, u32[]{:S(2)}) collective-permute-start(bf16[128,2048]{1,0:T(8,128)(2,1)} %shard_map.48), channel_id=1, source_target_pairs={{0,2},{1,3},{2,0},{3,1},{4,6},{5,7},{6,4},{7,5},{8,10},{9,11},{10,... | collective-permute-start | bytes 1572872 | tf_op jit(solution)/shard_map/ppermute | solution.py:168
  138.8 0.8 copy-start.3
  152.0 22.5 %collective-permute-start.11 = (bf16[128,2048]{1,0:T(8,128)(2,1)}, bf16[128,2048]{1,0:T(8,128)(2,1)S(1)}, u32[]{:S(2)}, u32[]{:S(2)}) collective-permute-start(bf16[128,2048]{1,0:T(8,128)(2,1)} %shard_map.49), channel_id=1, source_target_pairs={{0,1},{1,2},{2,3},{3,0},{4,5},{5,6},{6,7},{7,4},{8,9},{9,10},{10,1... | collective-permute-start | bytes 1572872 | tf_op jit(solution)/shard_map/ppermute | solution.py:168
  164.6 1.0 copy-start.2
  174.5 1.3 copy-start.1
